TPU v7x, 32 devices: a whole 2x2x4 slice. The times are simulated.
32 devices in a mesh: req: 4 (over y, x), exp: 8 (over z, core).
Axes of the slice: x: 2, y: 2, z: 4, core: 2. Of those that a mesh axis runs over, the one named last changes fastest.
Arguments:
- tokens: bfloat16 [4, 512, 2048], P('req', 'exp'), may hold values from -6 to 6
- cache: bfloat16 [4, 1024, 4096], P('req', None, 'exp'), may hold values from -64 to 64
- cache_len: int32 [4], P('req'), may hold values from 1 to 1024, 2560 in all
- attn_routes: int32 [4, 512, 2], P('req', 'exp'), may hold values from 0 to 7, all different within a row; in each aligned block of 64 rows (0 to 63, 64 to 127, ..., all dimensions but the last counted through in order) at most 24 rows name the same one
- mlp_routes: int32 [4, 512, 2], P('req', 'exp'), may hold values from 0 to 7, all different within a row; in each aligned block of 64 rows (0 to 63, 64 to 127, ..., all dimensions but the last counted through in order) at most 24 rows name the same one
- norm_attn: float32 [2048], replicated, may hold values from 0.5 to 1.5
- attn_router: bfloat16 [2048, 8], replicated, may hold values from -0.125 to 0.125
- w_query: bfloat16 [128, 2048, 128], P('exp'), may hold values from -0.125 to 0.125
- w_keyval: bfloat16 [2048, 4096], P(None, 'exp'), may hold values from -0.125 to 0.125
- w_out: bfloat16 [128, 128, 2048], P('exp'), may hold values from -0.125 to 0.125
- norm_mlp: float32 [2048], replicated, may hold values from 0.5 to 1.5
- mlp_router: bfloat16 [2048, 8], replicated, may hold values from -0.125 to 0.125
- w_gate: bfloat16 [8, 2048, 5632], P('exp'), may hold values from -0.125 to 0.125
- w_up: bfloat16 [8, 2048, 5632], P('exp'), may hold values from -0.125 to 0.125
- w_down: bfloat16 [8, 5632, 2048], P('exp'), may hold values from -0.078125 to 0.078125
Outputs:
- hidden_out: bfloat16 [4, 512, 2048], P('req', 'exp')
- cache_out: bfloat16 [4, 1536, 4096], P('req', None, 'exp')
Inputs may be any that keep to these rules, and one draw needn't show every extreme that they name: `attn_routes`: in each aligned block of 64 rows, no expert is named by more than 24 rows. `mlp_routes`: in each aligned block of 64 rows, no expert is named by more than 24 rows.
All inputs are finite; a program needn't handle non-finite values. No bound on the sum of `cache_len` on one device may be relied on, other than what follows from the above.
Results may differ from a plain program's by a relative error of at most 0.015.
The roundings to bfloat16 on the way count: a program that leaves them out, or rounds other values in their place, can miss the bound.
Values may be sent and summed in bfloat16 or wider, within the bound.
No kernel may reach another device: no remote copies, remote signals or barrier semaphores. Data moves between devices by JAX's collectives and lax.ppermute only.
A program may use at most 256 MiB of HBM per device.

v0:
```python
import math

import jax
import jax.numpy as jnp
from jax import lax
from jax.sharding import PartitionSpec as P

MOST = 24


epsilon = 1e-05
rope_base = 10000.0
masked_score = -1e30


def from_partner(value, axis, stride):
    mask = 2**stride
    pairs = [(source, source ^ mask) for source in range(lax.axis_size(axis))]
    return lax.ppermute(value, axis, pairs)


def rms_norm(values, gain_vec):
    widened = values.astype(jnp.float32)
    inv_rms = lax.rsqrt(jnp.mean(widened * widened, axis=-1, keepdims=True) + epsilon)
    return (widened * inv_rms * gain_vec).astype(jnp.bfloat16)


def rotate(values, position):
    half_dim = values.shape[-1] // 2
    inv_freq = rope_base ** (-jnp.arange(half_dim).astype(jnp.float32) / half_dim)
    angles = position.astype(jnp.float32)[..., None] * inv_freq
    cosine = jnp.cos(angles)
    sines = jnp.sin(angles)
    first_half = values[..., :half_dim]
    second_half = values[..., half_dim:]
    return jnp.concatenate(
        [first_half * cosine - second_half * sines, second_half * cosine + first_half * sines],
        axis=-1,
    )


def pick_gates(normed, router, routes):
    logits = jnp.dot(normed, router, preferred_element_type=jnp.float32)
    labels = jnp.arange(router.shape[1], dtype=jnp.int32)
    onehot = (routes[:, :, None] == labels[None, None, :]).astype(jnp.float32)
    chosen = jnp.sum(onehot * logits[:, None, :], axis=-1)
    return jax.nn.softmax(chosen, axis=-1)


def slot_tables(routes, gates, labels, rows_block, slot_count):
    row_total = routes.shape[0]
    block_count = row_total // rows_block
    matches = routes[:, :, None] == labels[None, None, :]
    member = jnp.any(matches, axis=1).astype(jnp.int32).reshape(block_count, rows_block, -1)
    weight = jnp.sum(jnp.where(matches, gates[:, :, None], 0.0), axis=1).reshape(
        block_count, rows_block, -1
    )
    ranking = jnp.cumsum(member, axis=1) - 1
    slot_ids = jnp.arange(slot_count, dtype=jnp.int32)
    onehot = ((member[..., None] > 0) & (ranking[..., None] == slot_ids)).astype(jnp.int32)
    local_row = jnp.arange(rows_block, dtype=jnp.int32)[None, :, None, None]
    token_ids = (
        jnp.sum(onehot * local_row, axis=1)
        + (jnp.arange(block_count, dtype=jnp.int32) * rows_block)[:, None, None]
    )
    shares = jnp.sum(onehot.astype(jnp.float32) * weight[..., None], axis=1)
    return (token_ids, shares)


def spread_rows(terms, token_ids, extent):
    term_part = terms.reshape(-1, terms.shape[-1])
    id_part = token_ids.reshape(-1)
    return jnp.zeros((extent, terms.shape[-1]), jnp.float32).at[id_part].add(term_part, mode="drop")


def attend(queries, query_pos, key_cache, value_cache, key_fresh, value_fresh, length):
    query_count = queries.shape[0]
    head_dim = queries.shape[1]
    factor = head_dim ** (-0.5)

    def absorb(state, key_block, value_block, visible):
        running_top, running_total, running_acc = state
        scores = jnp.dot(queries, key_block.T, preferred_element_type=jnp.float32) * factor
        scores = jnp.where(visible, scores, masked_score)
        new_top = jnp.maximum(running_top, jnp.max(scores, axis=1))
        fading = jnp.exp(running_top - new_top)
        weights = jnp.exp(scores - new_top[:, None])
        running_total = running_total * fading + jnp.sum(weights, axis=1)
        running_acc = running_acc * fading[:, None] + jnp.dot(
            weights.astype(jnp.bfloat16), value_block, preferred_element_type=jnp.float32
        )
        return (new_top, running_total, running_acc)

    state = (
        jnp.full((query_count,), masked_score, jnp.float32),
        jnp.zeros((query_count,), jnp.float32),
        jnp.zeros((query_count, head_dim), jnp.float32),
    )
    cache_span = math.gcd(512, key_cache.shape[0])

    def cache_step(step_idx, state):
        offset = step_idx * cache_span
        key_block = lax.dynamic_slice_in_dim(key_cache, offset, cache_span, 0)
        value_block = lax.dynamic_slice_in_dim(value_cache, offset, cache_span, 0)
        visible = (offset + jnp.arange(cache_span, dtype=jnp.int32))[None, :] < length
        return absorb(state, key_block, value_block, visible)

    state = lax.fori_loop(0, (length + cache_span - 1) // cache_span, cache_step, state)
    fresh_span = math.gcd(512, key_fresh.shape[0])
    for offset in range(0, key_fresh.shape[0], fresh_span):
        visible = (offset + jnp.arange(fresh_span, dtype=jnp.int32))[None, :] <= query_pos[:, None]
        state = absorb(
            state,
            key_fresh[offset : offset + fresh_span],
            value_fresh[offset : offset + fresh_span],
            visible,
        )
    running_top, running_total, running_acc = state
    return (running_acc / running_total[:, None]).astype(jnp.bfloat16)


def body(
    tokens,
    cache,
    cache_len,
    attn_routes,
    mlp_routes,
    norm_attn,
    attn_router,
    w_query,
    w_keyval,
    w_out,
    norm_mlp,
    mlp_router,
    w_gate,
    w_up,
    w_down,
):
    device_count = lax.axis_size("exp")
    position = lax.axis_index("exp")
    own_rows = tokens[0]
    rows_block = own_rows.shape[0]
    model_width = own_rows.shape[1]
    length = cache_len[0]
    slot_count = MOST
    normed = rms_norm(own_rows, norm_attn)
    group_normed, group_routes = (
        lax.all_gather(normed, "exp", axis=0, tiled=True),
        lax.all_gather(attn_routes[0], "exp", axis=0, tiled=True),
    )
    row_total = group_normed.shape[0]
    block_count = row_total // rows_block
    heads_here = w_query.shape[0]
    head_dim = w_query.shape[2]
    columns = w_keyval.shape[1]
    experts_attn = attn_router.shape[1]
    my_attn = jnp.reshape(position % experts_attn, (1,))
    new_pos = length + jnp.arange(row_total, dtype=jnp.int32)
    fresh_kv = jnp.dot(group_normed, w_keyval, preferred_element_type=jnp.float32)
    if columns < 2 * head_dim:
        is_key = position % 2 == 0
        fresh_kv = jnp.where(is_key, rotate(fresh_kv, new_pos), fresh_kv).astype(jnp.bfloat16)
    else:
        split_new = fresh_kv.reshape(row_total, columns // (2 * head_dim), 2, head_dim)
        rotated = rotate(split_new[:, :, 0], new_pos[:, None])
        fresh_kv = (
            jnp.stack([rotated, split_new[:, :, 1]], axis=2)
            .astype(jnp.bfloat16)
            .reshape(row_total, columns)
        )
    cache_limit = cache.shape[1]
    padded = jnp.concatenate([cache[0], jnp.zeros((row_total, columns), jnp.bfloat16)], axis=0)
    placed = lax.dynamic_update_slice(jnp.zeros_like(padded), fresh_kv, (length, jnp.int32(0)))
    slot_ids = jnp.arange(cache_limit + row_total, dtype=jnp.int32)
    cache_next = jnp.where((slot_ids < length)[:, None], padded, placed)
    group_cache = cache[0]
    group_fresh = fresh_kv
    for bit in range(experts_attn.bit_length() - 1):
        other_cache, other_fresh = from_partner((group_cache, group_fresh), "exp", bit)
        lower = position // (1 << bit) % 2 == 0
        group_cache = jnp.where(
            lower,
            jnp.concatenate([group_cache, other_cache], axis=1),
            jnp.concatenate([other_cache, group_cache], axis=1),
        )
        group_fresh = jnp.where(
            lower,
            jnp.concatenate([group_fresh, other_fresh], axis=1),
            jnp.concatenate([other_fresh, group_fresh], axis=1),
        )
    split_old = group_cache.reshape(cache_limit, heads_here, 2, head_dim)
    split_fresh = group_fresh.reshape(row_total, heads_here, 2, head_dim)
    attn_gates = pick_gates(group_normed, attn_router, group_routes)
    attn_tokens, attn_shares = slot_tables(
        group_routes, attn_gates, my_attn, rows_block, slot_count
    )
    token_flat = attn_tokens[:, 0, :].reshape(-1)
    share_flat = attn_shares[:, 0, :].reshape(-1)
    picked_rows = group_normed[token_flat]
    queries = jnp.einsum("sd,hdk->hsk", picked_rows, w_query, preferred_element_type=jnp.float32)
    queries = rotate(queries, (length + token_flat)[None, :]).astype(jnp.bfloat16)
    attend_heads = jax.vmap(attend, in_axes=(0, None, 1, 1, 1, 1, None))
    head_outs = attend_heads(
        queries,
        token_flat,
        split_old[:, :, 0],
        split_old[:, :, 1],
        split_fresh[:, :, 0],
        split_fresh[:, :, 1],
        length,
    )
    projected = jnp.einsum("hsk,hkd->sd", head_outs, w_out, preferred_element_type=jnp.float32)
    projected = (projected * share_flat[:, None]).reshape(block_count, slot_count, model_width)
    attn_ids = attn_tokens[:, 0, :]
    attn_own = lax.psum_scatter(
        spread_rows(projected, attn_ids, rows_block * lax.axis_size("exp")).astype(jnp.bfloat16),
        "exp",
        scatter_dimension=0,
        tiled=True,
    ).astype(jnp.float32)
    middle = lax.optimization_barrier(
        (own_rows.astype(jnp.float32) + attn_own).astype(jnp.bfloat16)
    )
    normed_mlp = rms_norm(middle, norm_mlp)
    experts_mlp = mlp_router.shape[1]
    split_count = device_count // experts_mlp
    my_expert = jnp.reshape(position // split_count, (1,))
    all_normed, all_routes = (
        lax.all_gather(normed_mlp, "exp", axis=0, tiled=True),
        lax.all_gather(mlp_routes[0], "exp", axis=0, tiled=True),
    )
    all_gates = pick_gates(all_normed, mlp_router, all_routes)
    mlp_tokens, mlp_shares = slot_tables(all_routes, all_gates, my_expert, rows_block, slot_count)
    inputs = all_normed[mlp_tokens.reshape(-1)]
    gate_part = jnp.dot(inputs, w_gate[0], preferred_element_type=jnp.float32)
    up_part = jnp.dot(inputs, w_up[0], preferred_element_type=jnp.float32)
    hidden = (jax.nn.silu(gate_part) * up_part).astype(jnp.bfloat16)
    slice_out = lax.optimization_barrier(
        jnp.dot(hidden, w_down[0], preferred_element_type=jnp.float32).astype(jnp.bfloat16)
    )
    weighted = (slice_out.astype(jnp.float32) * mlp_shares.reshape(-1)[:, None]).reshape(
        block_count, slot_count, model_width
    )
    mlp_ids = mlp_tokens[:, 0, :]
    mlp_own = lax.psum_scatter(
        spread_rows(weighted, mlp_ids, rows_block * lax.axis_size("exp")).astype(jnp.bfloat16),
        "exp",
        scatter_dimension=0,
        tiled=True,
    ).astype(jnp.float32)
    layer_out = (middle.astype(jnp.float32) + mlp_own).astype(jnp.bfloat16)
    return (layer_out[None], cache_next[None])


def solution(mesh):
    placed = (
        P("req", "exp", None),
        P("req", None, "exp"),
        P("req"),
        P("req", "exp", None),
        P("req", "exp", None),
        P(),
        P(),
        P("exp", None, None),
        P(None, "exp"),
        P("exp", None, None),
        P(),
        P(),
        P("exp", None, None),
        P("exp", None, None),
        P("exp", None, None),
    )
    return jax.shard_map(
        body,
        mesh=mesh,
        in_specs=placed,
        out_specs=(P("req", "exp", None), P("req", None, "exp")),
        check_vma=False,
    )
```

profile of v0, /device:TPU:0, one launch (start us, length us, event | category | flops | bytes accessed | tf_op | source)
XLA Modules:
  0.0 597.6 jit_solution(17848477500451785109)
XLA Ops:
  14.5 16.4 %all-gather = s32[1,512,2]{2,0,1:T(1,128)S(1)} all-gather(s32[1,64,2]{2,0,1:T(1,128)S(1)} %copy.70), channel_id=2, replica_groups=mesh['req'=4,'exp'=8] {'exp'}, dimensions={1}, use_global_device_ids=true | all-gather | bytes 4608 | tf_op jit(solution)/shard_map/all_gather | solution.py:149
  31.8 15.1 %all-gather.1 = s32[1,512,2]{2,0,1:T(1,128)S(1)} all-gather(s32[1,64,2]{2,0,1:T(1,128)S(1)} %copy.88), channel_id=3, replica_groups=mesh['req'=4,'exp'=8] {'exp'}, dimensions={1}, use_global_device_ids=true | all-gather | bytes 4608 | tf_op jit(solution)/shard_map/all_gather | solution.py:230
  60.8 39.0 %collective-permute-done.1 = bf16[1024,1024]{1,0:T(8,128)(2,1)} collective-permute-done((bf16[1024,1024]{1,0:T(8,128)(2,1)}, bf16[1024,1024]{1,0:T(8,128)(2,1)}, u32[]{:S(2)}, u32[]{:S(2)}) %collective-permute-start.1) | collective-permute-done | bytes 2097184 | tf_op jit(solution)/shard_map/ppermute | solution.py:19
  99.8 6.7 %maximum_select_fusion.2 = bf16[1024,2048]{1,0:T(8,128)(2,1)} fusion(bf16[1024,1024]{1,0:T(8,128)(2,1)} %collective-permute-done.1, bf16[1024,1024]{1,0:T(8,128)(2,1)} %maximum_select_fusion.5, pred[]{:T(512)S(6)} %eq.114), kind=kLoop, calls=%fused_computation.44 | loop fusion | flops 18874368 | bytes 8388609 | tf_op jit(solution)/shard_map/jit(_where)/select_n | solution.py:181
  112.9 5.1 maximum_select_fusion.1
  129.1 5.4 convolution_bitcast_fusion.1
  137.1 84.4 %collective-permute-done.4 = bf16[512,1024]{0,1:T(8,128)(2,1)S(1)} collective-permute-done((bf16[512,1024]{0,1:T(8,128)(2,1)S(1)}, bf16[512,1024]{0,1:T(8,128)(2,1)S(1)}, u32[]{:S(2)}, u32[]{:S(2)}) %collective-permute-start.4) | collective-permute-done | bytes 1048608 | tf_op jit(solution)/shard_map/ppermute | solution.py:19
  227.7 108.2 %collective-permute-done.2 = bf16[1024,2048]{1,0:T(8,128)(2,1)} collective-permute-done((bf16[1024,2048]{1,0:T(8,128)(2,1)}, bf16[1024,2048]{1,0:T(8,128)(2,1)}, u32[]{:S(2)}, u32[]{:S(2)}) %collective-permute-start.2) | collective-permute-done | bytes 4194336 | tf_op jit(solution)/shard_map/ppermute | solution.py:19
  335.9 6.4 %copy.75 = bf16[1024,2048]{0,1:T(8,128)(2,1)} copy(bf16[1024,2048]{1,0:T(8,128)(2,1)} %collective-permute-done.2) | data formatting | bytes 8388608 | tf_op jit(solution)/shard_map/ppermute | solution.py:19
  342.3 6.6 %maximum_select_fusion = bf16[1024,16,2,128]{0,3,2,1:T(8,128)(2,1)S(1)} fusion(bf16[1024,8,2,128]{0,3,2,1:T(8,128)(2,1)} %bitcast.160, bf16[1024,8,2,128]{0,3,2,1:T(8,128)(2,1)} %maximum_select_fusion.1, pred[]{:T(512)S(6)} %eq.113), kind=kLoop, calls=%fused_computation.33 | loop fusion | flops 12582912 | bytes 16777216 | tf_op jit(solution)/shard_map/jit(_where)/select_n | solution.py:181
  353.9 55.3 %while.16 = (s32[]{:T(128)}, f32[16,192]{1,0:T(8,128)S(1)}, f32[16,192]{1,0:T(8,128)S(1)}, f32[16,192,128]{2,1,0:T(8,128)}, s32[]{:T(128)}, /*index=5*/s32[]{:T(...) while((s32[]{:T(128)}, f32[16,192]{1,0:T(8,128)S(1)}, ...), condition=%wide.region_7.8_spmd, body=%wide.region_4.7_spmd.sunk | while | flops 823401472 | bytes 69142768 | solution.py:108
  354.7 6.4 %constant_dynamic-slice_fusion.3 = (bf16[512,16,128]{0,2,1:T(8,128)(2,1)S(1)}, bf16[512,16,128]{0,2,1:T(8,128)(2,1)}) fusion(bf16[1024,16,128]{0,2,1:T(8,128)(2,1)} %get-tuple-element.252, s32[]{:T(128)S(1)} %bitcast.175, bf16[1024,16,128]{0,2,1:T(8,128)(2,1)} %get-tuple-element.250), kind=kLoop, calls=%fused_computation.23.clone.1 | loop fusion | bytes 8388612 | tf_op jit(solution)/shard_map/vmap()/while
  374.6 6.9 %multiply_add_fusion.7 = f32[16,192,128]{2,1,0:T(8,128)} fusion(f32[16,192,128]{2,1,0:T(8,128)} %get-tuple-element.233, bf16[512,16,128]{2,0,1:T(8,128)(2,1)} %copy.105, f32[16,512,192]{1,2,0:T(8,128)} %copy-done.2, f32[16,192]{1,0:T(8,128)S(1)} %max.10, pred[512]{0:T(512)(128)(4,1)S(1)} %add_compare_fusion.2, f32[16,192]{1,0:T(8,128)S(1)} %get-tuple-element.215), kind=kOutput, calls=%fused_computation.18.clone.1 | convolution fusion | flops 409731072 | bytes 11559424 | tf_op jit(solution)/shard_map/vmap()/while/body/dot_general | solution.py:89
  382.3 6.1 %constant_dynamic-slice_fusion.3 = (bf16[512,16,128]{0,2,1:T(8,128)(2,1)S(1)}, bf16[512,16,128]{0,2,1:T(8,128)(2,1)}) fusion(bf16[1024,16,128]{0,2,1:T(8,128)(2,1)} %get-tuple-element.252, s32[]{:T(128)S(1)} %bitcast.175, bf16[1024,16,128]{0,2,1:T(8,128)(2,1)} %get-tuple-element.250), kind=kLoop, calls=%fused_computation.23.clone.1 | loop fusion | bytes 8388612 | tf_op jit(solution)/shard_map/vmap()/while
  401.9 6.9 %multiply_add_fusion.7 = f32[16,192,128]{2,1,0:T(8,128)} fusion(f32[16,192,128]{2,1,0:T(8,128)} %get-tuple-element.233, bf16[512,16,128]{2,0,1:T(8,128)(2,1)} %copy.105, f32[16,512,192]{1,2,0:T(8,128)} %copy-done.2, f32[16,192]{1,0:T(8,128)S(1)} %max.10, pred[512]{0:T(512)(128)(4,1)S(1)} %add_compare_fusion.2, f32[16,192]{1,0:T(8,128)S(1)} %get-tuple-element.215), kind=kOutput, calls=%fused_computation.18.clone.1 | convolution fusion | flops 409731072 | bytes 11559424 | tf_op jit(solution)/shard_map/vmap()/while/body/dot_general | solution.py:89
  409.3 4.3 maximum_select_fusion.3
  420.5 10.8 %fusion.39 = f32[192,2048]{1,0:T(8,128)} fusion(bf16[16,128,2048]{2,1,0:T(8,128)(2,1)} %param.26, f32[16,192,128]{2,1,0:T(8,128)S(1)} %copy-done.11, bf16[512,16,2,128]{0,3,1,2:T(8,128)(2,1)} %copy-done.8, f32[16,192,512]{2,1,0:T(8,128)} %copy-done.5, f32[16,192]{1,0:T(8,128)S(1)} %max.8, pred[192,512]{1,0:T(8,128)(4,1)S(1)} %iota_compare_fusion, ...), kind=kOutput, calls=%fused_computation.52 | convolution fusion | flops 2021523456 | bytes 20058880 | tf_op jit(solution)/shard_map/hsk,hkd->sd/dot_general | solution.py:212
  431.3 5.9 scatter_custom_fusion
  441.2 35.1 %reduce-scatter.3.cloned.1.call-done = bf16[64,2048]{1,0:T(8,128)(2,1)} async-done(((bf16[512,2048]{1,0:T(8,128)(2,1)}), bf16[64,2048]{1,0:T(8,128)(2,1)}) %reduce-scatter.3.cloned.1.call-update) | async-done | bytes 262160 | tf_op jit(solution)/shard_map/reduce_scatter | solution.py:215
  478.6 27.7 %all-gather.7.cloned.1.call-done = bf16[512,2048]{1,0:T(8,128)(2,1)} async-done(((bf16[64,2048]{1,0:T(8,128)(2,1)}), bf16[512,2048]{1,0:T(8,128)(2,1)}) %all-gather.7.cloned.1.call-update) | async-done | bytes 2097168 | tf_op jit(solution)/shard_map/all_gather | solution.py:229
  510.9 12.0 %fusion.22 = f32[192,5632]{1,0:T(8,128)} fusion(bf16[192,2048]{1,0:T(8,128)(2,1)S(1)} %gather_fusion.1, bf16[1,2048,5632]{2,1,0:T(8,128)(2,1)} %param.29), kind=kOutput, calls=%fused_computation.31 | convolution fusion | flops 4429185024 | bytes 28180480 | tf_op jit(solution)/shard_map/dot_general | solution.py:235
  522.9 20.6 %fusion.40 = bf16[192,2048]{1,0:T(8,128)(2,1)S(1)} fusion(bf16[1,5632,2048]{2,1,0:T(8,128)(2,1)} %param.31, bf16[192,2048]{1,0:T(8,128)(2,1)} %copy-done.12, bf16[1,2048,5632]{2,1,0:T(8,128)(2,1)} %param.30, f32[192,5632]{1,0:T(8,128)} %fusion.22), kind=kOutput, calls=%fused_computation.53 | convolution fusion | flops 8865251328 | bytes 52035584 | tf_op jit(solution)/shard_map/dot_general | solution.py:239
  544.6 5.2 scatter_custom_fusion.1
  564.3 24.8 %reduce-scatter.5.cloned.1.call-done = bf16[64,2048]{1,0:T(8,128)(2,1)} async-done(((bf16[512,2048]{1,0:T(8,128)(2,1)}), bf16[64,2048]{1,0:T(8,128)(2,1)}) %reduce-scatter.5.cloned.1.call-update) | async-done | bytes 262160 | tf_op jit(solution)/shard_map/reduce_scatter | solution.py:245
  (178 shorter events, 115.9 us)
Async XLA Ops:
  7.2 110.8 %copy-start = (bf16[2048,512]{1,0:T(8,128)(2,1)S(1)}, bf16[2048,512]{1,0:T(8,128)(2,1)}, u32[]{:S(2)}) copy-start(bf16[2048,512]{1,0:T(8,128)(2,1)} %param.25) | copy-start | bytes 6291460
  7.2 40.8 %copy-start.6 = (bf16[1,1024,512]{2,1,0:T(8,128)(2,1)S(1)}, bf16[1,1024,512]{2,1,0:T(8,128)(2,1)}, u32[]{:S(2)}) copy-start(bf16[1,1024,512]{2,1,0:T(8,128)(2,1)} %param.18) | copy-start | bytes 3145732
  7.2 110.8 %all-gather.5.cloned.1.call-start = ((), (), s32[]{:S(2)}) async-start(), calls=%async_computation.2 | async-start | bytes 2359296 | tf_op jit(solution)/shard_map/all_gather | solution.py:148
  7.2 40.8 %collective-permute-start = (bf16[1024,512]{1,0:T(8,128)(2,1)}, bf16[1024,512]{1,0:T(8,128)(2,1)}, u32[]{:S(2)}, u32[]{:S(2)}) collective-permute-start(bf16[1024,512]{1,0:T(8,128)(2,1)} %bitcast.161), channel_id=1, source_target_pairs={{0,1},{1,0},{2,3},{3,2},{4,5},{5,4},{6,7},{7,6},{8,9},{9,8},{10,11... | collective-permute-start | bytes 3145736 | tf_op jit(solution)/shard_map/ppermute | solution.py:19
  10.7 465.6 %reduce-scatter.3.cloned.1.call-start = ((), (), s32[]{:S(2)}) async-start(), calls=%async_computation.3 | async-start | bytes 2359296 | tf_op jit(solution)/shard_map/reduce_scatter | solution.py:215
  46.9 7.0 %copy-start.15 = (s32[1,512,2]{1,2,0:T(2,128)}, s32[1,512,2]{1,2,0:T(2,128)S(1)}, u32[]{:S(2)}) copy-start(s32[1,512,2]{1,2,0:T(2,128)S(1)} %copy.89) | copy-start | bytes 12292
  51.6 48.2 %collective-permute-start.1 = (bf16[1024,1024]{1,0:T(8,128)(2,1)}, bf16[1024,1024]{1,0:T(8,128)(2,1)}, u32[]{:S(2)}, u32[]{:S(2)}) collective-permute-start(bf16[1024,1024]{1,0:T(8,128)(2,1)} %maximum_select_fusion.5), channel_id=1, source_target_pairs={{0,2},{1,3},{2,0},{3,1},{4,6},{5,7},{6,4},{7,5},{8,10},{9,11},{10,... | collective-permute-start | bytes 6291464 | tf_op jit(solution)/shard_map/ppermute | solution.py:19
  106.5 229.4 %collective-permute-start.2 = (bf16[1024,2048]{1,0:T(8,128)(2,1)}, bf16[1024,2048]{1,0:T(8,128)(2,1)}, u32[]{:S(2)}, u32[]{:S(2)}) collective-permute-start(bf16[1024,2048]{1,0:T(8,128)(2,1)} %maximum_select_fusion.2), channel_id=1, source_target_pairs={{0,4},{1,5},{2,6},{3,7},{4,0},{5,1},{6,2},{7,3},{8,12},{9,13},{10,... | collective-permute-start | bytes 12582920 | tf_op jit(solution)/shard_map/ppermute | solution.py:19
  121.2 4.5 collective-permute-start.3
  127.3 7.3 %copy-start.13 = (f32[192,64]{1,0:T(8,128)S(1)}, f32[192,64]{1,0:T(8,128)}, u32[]{:S(2)}) copy-start(f32[192,64]{1,0:T(8,128)} %get-tuple-element.140) | copy-start | bytes 147460
  127.3 7.3 %copy-start.14 = (f32[192,64]{1,0:T(8,128)S(1)}, f32[192,64]{1,0:T(8,128)}, u32[]{:S(2)}) copy-start(f32[192,64]{1,0:T(8,128)} %get-tuple-element.141) | copy-start | bytes 147460
  127.3 94.2 %collective-permute-start.4 = (bf16[512,1024]{0,1:T(8,128)(2,1)S(1)}, bf16[512,1024]{0,1:T(8,128)(2,1)S(1)}, u32[]{:S(2)}, u32[]{:S(2)}) collective-permute-start(bf16[512,1024]{0,1:T(8,128)(2,1)S(1)} %maximum_select_fusion.9), channel_id=1, source_target_pairs={{0,2},{1,3},{2,0},{3,1},{4,6},{5,7},{6,4},{7,5},{8,10},{9,11},{10,... | collective-permute-start | bytes 3145736 | tf_op jit(solution)/shard_map/ppermute | solution.py:19
  223.5 185.8 %collective-permute-start.5 = (bf16[512,2048]{0,1:T(8,128)(2,1)}, bf16[512,2048]{0,1:T(8,128)(2,1)}, u32[]{:S(2)}, u32[]{:S(2)}) collective-permute-start(bf16[512,2048]{0,1:T(8,128)(2,1)} %maximum_select_fusion.7), channel_id=1, source_target_pairs={{0,4},{1,5},{2,6},{3,7},{4,0},{5,1},{6,2},{7,3},{8,12},{9,13},{10,... | collective-permute-start | bytes 6291464 | tf_op jit(solution)/shard_map/ppermute | solution.py:19
  437.2 39.1 %copy-start.10 = (bf16[1,64,2048]{2,1,0:T(8,128)(2,1)S(1)}, bf16[1,64,2048]{2,1,0:T(8,128)(2,1)}, u32[]{:S(2)}) copy-start(bf16[1,64,2048]{2,1,0:T(8,128)(2,1)} %param.17) | copy-start | bytes 786436
  437.2 40.3 %copy-start.23 = (f32[2048]{0:T(1024)S(1)}, f32[2048]{0:T(1024)}, u32[]{:S(2)}) copy-start(f32[2048]{0:T(1024)} %param.27) | copy-start | bytes 24580
  441.1 65.1 %all-gather.7.cloned.1.call-start = ((), (), s32[]{:S(2)}) async-start(), calls=%async_computation.4 | async-start | bytes 2359296 | tf_op jit(solution)/shard_map/all_gather | solution.py:229
  478.3 110.8 %reduce-scatter.5.cloned.1.call-start = ((), (), s32[]{:S(2)}) async-start(), calls=%async_computation.5 | async-start | bytes 2359296 | tf_op jit(solution)/shard_map/reduce_scatter | solution.py:245
  522.9 20.7 %copy-start.4 = (bf16[512,2048]{1,0:T(8,128)(2,1)S(1)}, bf16[512,2048]{1,0:T(8,128)(2,1)}, u32[]{:S(2)}) copy-start(bf16[512,2048]{1,0:T(8,128)(2,1)} %all-gather.7.cloned.1.call-done) | copy-start | bytes 6291460
  522.9 20.7 %copy-start.20 = (bf16[2048,8]{0,1:T(8,128)(2,1)S(1)}, bf16[2048,8]{0,1:T(8,128)(2,1)}, u32[]{:S(2)}) copy-start(bf16[2048,8]{0,1:T(8,128)(2,1)} %param.28) | copy-start | bytes 98308
  522.9 21.3 %copy-start.16 = (s32[1,512,2]{1,2,0:T(2,128)S(1)}, s32[1,512,2]{1,2,0:T(2,128)}, u32[]{:S(2)}) copy-start(s32[1,512,2]{1,2,0:T(2,128)} %copy-done.15) | copy-start | bytes 12292
  522.9 21.5 %copy-start.18 = (s32[8,64]{1,0:T(8,128)S(1)}, s32[8,64]{1,0:T(8,128)}, u32[]{:S(2)}) copy-start(s32[8,64]{1,0:T(8,128)} %copy-done.17) | copy-start | bytes 6148
  522.9 21.5 %copy-start.22 = (pred[8,64]{1,0:T(8,128)(4,1)S(1)}, pred[8,64]{1,0:T(8,128)(4,1)}, u32[]{:S(2)}) copy-start(pred[8,64]{1,0:T(8,128)(4,1)} %copy-done.21) | copy-start | bytes 1540
  553.6 7.6 %copy-start.7 = (bf16[1,1024,512]{2,1,0:T(8,128)(2,1)S(1)}, bf16[1,1024,512]{2,1,0:T(8,128)(2,1)}, u32[]{:S(2)}) copy-start(bf16[1,1024,512]{2,1,0:T(8,128)(2,1)} %param.18) | copy-start | bytes 3145732
  553.7 37.2 %copy-start.1 = (bf16[2048,512]{1,0:T(8,128)(2,1)S(1)}, bf16[2048,512]{1,0:T(8,128)(2,1)}, u32[]{:S(2)}) copy-start(bf16[2048,512]{1,0:T(8,128)(2,1)} %param.25) | copy-start | bytes 6291460
  (11 other events, 30.4 us)
Sparse Core Ops, SparseCore 0:
  10.8 34.0 all-gather.4
  441.2 35.0 reduce-scatter.2
  478.5 27.7 all-gather.6
  553.8 35.3 reduce-scatter.4
where the time goes:
time: 603 us; the launch traced here: 598 us
  waiting for transfers between devices  319 us (53%)
  other arithmetic  76.5 us (13%)
  matrix products  73.7 us (12%)
  local copies, waits for them, and re-layouts  71.7 us (12%)
  blocking collectives  31.5 us (5%)
  between operations  15.2 us (3%)
  starting transfers between devices  9.3 us (2%)
    ppermute x6, waiting for transfers between devices, from_partner(): return lax.ppermute(value, axis, pairs)  232 us
    reduce_scatter x1, waiting for transfers between devices, body(): lax.psum_scatter(spread_rows(projected, attn_ids, rows_block * lax.axis_s...  35.1 us
    while x12, local copies, waits for them, and re-layouts  30.4 us
    all_gather x1, waiting for transfers between devices, body(): lax.all_gather(normed_mlp, 'exp', axis=0, tiled=True)  27.7 us
    select_n x5, other arithmetic, body(): jnp.where(lower, jnp.concatenate([group_cache, other_cache], axis=1), jnp...  25.2 us
    reduce_scatter x1, waiting for transfers between devices, body(): lax.psum_scatter(spread_rows(weighted, mlp_ids, rows_block * lax.axis_siz...  24.8 us
    dot_general x1, matrix products, body(): jnp.dot(hidden, w_down[0], preferred_element_type=jnp.float32)  20.6 us
    all_gather x1, blocking collectives, body(): lax.all_gather(attn_routes[0], 'exp', axis=0, tiled=True)  16.4 us
  transfers between devices with their start and end apart: 10, of which 6 were waited for; matrix products, arithmetic and copies ran while one was open for 22% of the time, Pallas kernels for 0%

commit v1 on v0

--- a/solution.py
+++ b/solution.py
@@ -119,7 +119,178 @@
     return (running_acc / running_total[:, None]).astype(jnp.bfloat16)
 
 
+def local_slots(routes, labels, slot_count):
+    matches = routes[:, :, None] == labels[None, None, :]
+    member = jnp.any(matches, axis=1).astype(jnp.int32)
+    ranking = jnp.cumsum(member, axis=0) - 1
+    slot_ids = jnp.arange(slot_count, dtype=jnp.int32)
+    onehot = ((member[..., None] > 0) & (ranking[..., None] == slot_ids)).astype(jnp.int32)
+    rows = jnp.arange(routes.shape[0], dtype=jnp.int32)[:, None, None]
+    return jnp.sum(onehot * rows, axis=0)
+
+
+def route_slots(routes, label_count):
+    labels = jnp.arange(label_count, dtype=jnp.int32)
+    member = jnp.any(routes[:, :, None] == labels[None, None, :], axis=1).astype(jnp.int32)
+    ranking = jnp.cumsum(member, axis=0) - 1
+    return jnp.take_along_axis(ranking, routes, axis=1)
+
+
+def combine(received, routes, gates, slots, split_count):
+    slot_count = received.shape[1]
+    flat = received.reshape(-1, received.shape[-1])
+    total = jnp.zeros((routes.shape[0], received.shape[-1]), jnp.float32)
+    for route in range(routes.shape[1]):
+        expert = routes[:, route]
+        part = jnp.zeros_like(total)
+        for piece in range(split_count):
+            index = (expert * split_count + piece) * slot_count + slots[:, route]
+            part = part + flat[index].astype(jnp.float32)
+        total = total + part * gates[:, route][:, None]
+    return total
+
+
+def head_attention(queries, query_pos, keys, values, length, cache_limit):
+    factor = queries.shape[-1] ** (-0.5)
+    scores = jnp.einsum("hqk,hsk->hqs", queries, keys, preferred_element_type=jnp.float32) * factor
+    slot_ids = jnp.arange(keys.shape[1], dtype=jnp.int32)[None, :]
+    visible = jnp.where(
+        slot_ids < cache_limit, slot_ids < length, slot_ids - cache_limit <= query_pos[:, None]
+    )
+    scores = jnp.where(visible[None], scores, masked_score)
+    top = jnp.max(scores, axis=-1, keepdims=True)
+    weights = jnp.exp(scores - top)
+    total = jnp.sum(weights, axis=-1, keepdims=True)
+    summed = jnp.einsum(
+        "hqs,hsk->hqk", weights.astype(jnp.bfloat16), values, preferred_element_type=jnp.float32
+    )
+    return (summed / total).astype(jnp.bfloat16)
+
+
 def body(
+    tokens,
+    cache,
+    cache_len,
+    attn_routes,
+    mlp_routes,
+    norm_attn,
+    attn_router,
+    w_query,
+    w_keyval,
+    w_out,
+    norm_mlp,
+    mlp_router,
+    w_gate,
+    w_up,
+    w_down,
+):
+    device_count = lax.axis_size("exp")
+    position = lax.axis_index("exp")
+    own_rows = tokens[0]
+    rows_block = own_rows.shape[0]
+    model_width = own_rows.shape[1]
+    length = cache_len[0]
+    slot_count = MOST
+    heads_here = w_query.shape[0]
+    head_dim = w_query.shape[2]
+    columns = w_keyval.shape[1]
+    experts_attn = attn_router.shape[1]
+    kv_heads = columns * device_count // (2 * head_dim)
+    fast_attn = (
+        device_count == experts_attn and heads_here == kv_heads and columns % (2 * head_dim) == 0
+    )
+    if not fast_attn:
+        return base_body(
+            tokens, cache, cache_len, attn_routes, mlp_routes, norm_attn, attn_router, w_query,
+            w_keyval, w_out, norm_mlp, mlp_router, w_gate, w_up, w_down,
+        )
+    normed = rms_norm(own_rows, norm_attn)
+    route_rows = jnp.zeros((16, model_width), jnp.bfloat16)
+    route_rows = route_rows.at[0, : 2 * rows_block].set(
+        attn_routes[0].reshape(-1).astype(jnp.bfloat16)
+    )
+    gathered = lax.all_gather(
+        jnp.concatenate([normed, route_rows], axis=0), "exp", axis=0, tiled=False
+    )
+    group_normed = gathered[:, :rows_block].reshape(-1, model_width)
+    group_routes = (
+        gathered[:, rows_block, : 2 * rows_block].astype(jnp.int32).reshape(-1, 2)
+    )
+    row_total = group_normed.shape[0]
+    block_count = row_total // rows_block
+    new_pos = length + jnp.arange(row_total, dtype=jnp.int32)
+    fresh_kv = jnp.dot(group_normed, w_keyval, preferred_element_type=jnp.float32)
+    split_new = fresh_kv.reshape(row_total, columns // (2 * head_dim), 2, head_dim)
+    rotated = rotate(split_new[:, :, 0], new_pos[:, None])
+    fresh_kv = (
+        jnp.stack([rotated, split_new[:, :, 1]], axis=2)
+        .astype(jnp.bfloat16)
+        .reshape(row_total, columns)
+    )
+    cache_limit = cache.shape[1]
+    padded = jnp.concatenate([cache[0], jnp.zeros((row_total, columns), jnp.bfloat16)], axis=0)
+    placed = lax.dynamic_update_slice(jnp.zeros_like(padded), fresh_kv, (length, jnp.int32(0)))
+    slot_ids = jnp.arange(cache_limit + row_total, dtype=jnp.int32)
+    cache_next = jnp.where((slot_ids < length)[:, None], padded, placed)
+
+    all_labels = jnp.arange(experts_attn, dtype=jnp.int32)
+    blocks_routes = group_routes.reshape(block_count, rows_block, -1)
+    slot_tokens = jax.vmap(lambda r: local_slots(r, all_labels, slot_count))(blocks_routes)
+    slot_tokens = slot_tokens + (jnp.arange(block_count, dtype=jnp.int32) * rows_block)[:, None, None]
+    expert_tokens = jnp.swapaxes(slot_tokens, 0, 1).reshape(experts_attn, -1)
+    my_tokens = expert_tokens[position]
+    picked_rows = group_normed[my_tokens]
+    queries = jnp.einsum("sd,hdk->hsk", picked_rows, w_query, preferred_element_type=jnp.float32)
+    queries = rotate(queries, (length + my_tokens)[None, :]).astype(jnp.bfloat16)
+    heads_local = columns // (2 * head_dim)
+    query_slots = queries.shape[1]
+    send_q = queries.reshape(device_count, heads_local, query_slots, head_dim)
+    recv_q = lax.all_to_all(send_q, "exp", 0, 0, tiled=True)
+    recv_q = jnp.swapaxes(recv_q, 0, 1).reshape(heads_local, device_count * query_slots, head_dim)
+    query_pos = expert_tokens.reshape(-1)
+    split_old = cache[0].reshape(cache_limit, heads_local, 2, head_dim)
+    split_fresh = fresh_kv.reshape(row_total, heads_local, 2, head_dim)
+    keys = jnp.swapaxes(jnp.concatenate([split_old[:, :, 0], split_fresh[:, :, 0]], axis=0), 0, 1)
+    values = jnp.swapaxes(jnp.concatenate([split_old[:, :, 1], split_fresh[:, :, 1]], axis=0), 0, 1)
+    head_outs = head_attention(recv_q, query_pos, keys, values, length, cache_limit)
+    send_o = jnp.swapaxes(
+        head_outs.reshape(heads_local, device_count, query_slots, head_dim), 0, 1
+    )
+    recv_o = lax.all_to_all(send_o, "exp", 0, 0, tiled=True)
+    recv_o = recv_o.reshape(heads_here, query_slots, head_dim)
+    projected = jnp.einsum("hsk,hkd->sd", recv_o, w_out, preferred_element_type=jnp.float32)
+    send_p = projected.astype(jnp.bfloat16).reshape(block_count, slot_count, model_width)
+    recv_p = lax.all_to_all(send_p, "exp", 0, 0, tiled=True)
+    own_attn_routes = attn_routes[0]
+    attn_gates = pick_gates(normed, attn_router, own_attn_routes)
+    attn_own = combine(
+        recv_p, own_attn_routes, attn_gates, route_slots(own_attn_routes, experts_attn), 1
+    )
+    middle = (own_rows.astype(jnp.float32) + attn_own).astype(jnp.bfloat16)
+    normed_mlp = rms_norm(middle, norm_mlp)
+    experts_mlp = mlp_router.shape[1]
+    split_count = device_count // experts_mlp
+    own_mlp_routes = mlp_routes[0]
+    mlp_gates = pick_gates(normed_mlp, mlp_router, own_mlp_routes)
+    mlp_tokens = local_slots(own_mlp_routes, jnp.arange(experts_mlp, dtype=jnp.int32), slot_count)
+    dest_tokens = jnp.repeat(mlp_tokens, split_count, axis=0)
+    send_m = normed_mlp[dest_tokens.reshape(-1)].reshape(device_count, slot_count, model_width)
+    inputs = lax.all_to_all(send_m, "exp", 0, 0, tiled=True).reshape(-1, model_width)
+    gate_part = jnp.dot(inputs, w_gate[0], preferred_element_type=jnp.float32)
+    up_part = jnp.dot(inputs, w_up[0], preferred_element_type=jnp.float32)
+    hidden = (jax.nn.silu(gate_part) * up_part).astype(jnp.bfloat16)
+    slice_out = jnp.dot(hidden, w_down[0], preferred_element_type=jnp.float32).astype(jnp.bfloat16)
+    recv_m = lax.all_to_all(
+        slice_out.reshape(device_count, slot_count, model_width), "exp", 0, 0, tiled=True
+    )
+    mlp_own = combine(
+        recv_m, own_mlp_routes, mlp_gates, route_slots(own_mlp_routes, experts_mlp), split_count
+    )
+    layer_out = (middle.astype(jnp.float32) + mlp_own).astype(jnp.bfloat16)
+    return (layer_out[None], cache_next[None])
+
+
+def base_body(
     tokens,
     cache,
     cache_len,

time: 603 us -> 278 us (0.46)
  waiting for transfers between devices: 319 us -> 114 us
  other arithmetic: 76.5 us -> 30.1 us
  local copies, waits for them, and re-layouts: 71.7 us -> 31.1 us
  blocking collectives: 31.5 us -> 0 us
  starting transfers between devices: 9.3 us -> 19.1 us
  matrix products: 73.7 us -> 67.2 us
    ppermute x6 -> x0, waiting for transfers between devices: 232 us -> none  [from_partner(): return lax.ppermute(value, axis, pairs)]
    all_to_all x0 -> x5, waiting for transfers between devices: none -> 85.8 us  [the longest x1 20.8 us: body(): recv_p = lax.all_to_all(send_p, 'exp', 0, 0, tiled=True)]
    reduce_scatter x2 -> x0, waiting for transfers between devices: 59.9 us -> none  [the longest x1 35.1 us: body(): lax.psum_scatter(spread_rows(projected, attn_ids, rows_block * lax.axis_s...]
    select_n x11 -> x7, other arithmetic: 36.3 us -> 3.38 us  [the longest x1 3.32 us: head_attention(): jnp.where(slot_ids < cache_limit, slot_ids < length, slot_ids - cache_lim...]
    all_gather x2 -> x0, blocking collectives: 31.5 us -> none  [the longest x1 16.4 us: body(): lax.all_gather(attn_routes[0], 'exp', axis=0, tiled=True)]
    while x12 -> x0, local copies, waits for them, and re-layouts: 30.4 us -> none
    all_to_all x0 -> x5, starting transfers between devices: none -> 19.1 us  [the longest x1 4.42 us: body(): lax.all_to_all(send_m, 'exp', 0, 0, tiled=True).reshape(-1, model_width)]
    ppermute x3 -> x0, local copies, waits for them, and re-layouts: 12 us -> none  [from_partner(): return lax.ppermute(value, axis, pairs)]
  transfers between devices with their start and end apart: 10 -> 6, of which waited for: 6 -> 6; matrix products, arithmetic and copies ran while one was open for 22% -> 9% of each run, Pallas kernels for 0% -> 0%
where the time goes in v1:
time: 278 us; the launch traced here: 277 us
  waiting for transfers between devices  114 us (41%)
  matrix products  67.2 us (24%)
  local copies, waits for them, and re-layouts  31.1 us (11%)
  other arithmetic  30.1 us (11%)
  starting transfers between devices  19.1 us (7%)
  between operations  15.3 us (6%)
    all_gather x1, waiting for transfers between devices, body(): lax.all_gather(jnp.concatenate([normed, route_rows], axis=0), 'exp', axis...  28 us
    dot_general x1, matrix products, body(): jnp.dot(hidden, w_down[0], preferred_element_type=jnp.float32)  21.3 us
    all_to_all x1, waiting for transfers between devices, body(): recv_p = lax.all_to_all(send_p, 'exp', 0, 0, tiled=True)  20.8 us
    all_to_all x1, waiting for transfers between devices, body(): recv_o = lax.all_to_all(send_o, 'exp', 0, 0, tiled=True)  18.3 us
    all_to_all x1, waiting for transfers between devices, body(): lax.all_to_all(slice_out.reshape(device_count, slot_count, model_width),...  17.7 us
    all_to_all x1, waiting for transfers between devices, body(): recv_q = lax.all_to_all(send_q, 'exp', 0, 0, tiled=True)  15.3 us
    dot_general x1, matrix products, body(): gate_part = jnp.dot(inputs, w_gate[0], preferred_element_type=jnp.float32)  14.4 us
    all_to_all x1, waiting for transfers between devices, body(): lax.all_to_all(send_m, 'exp', 0, 0, tiled=True).reshape(-1, model_width)  13.6 us
  transfers between devices with their start and end apart: 6, of which 6 were waited for; matrix products, arithmetic and copies ran while one was open for 9% of the time, Pallas kernels for 0%

profile of v1, /device:TPU:0, one launch (start us, length us, event | category | flops | bytes accessed | tf_op | source)
XLA Modules:
  0.0 276.5 jit_solution(10235566921703914232)
XLA Ops:
  11.9 4.0 %copy.111 = bf16[512,2048]{1,0:T(8,128)(2,1)} copy(bf16[512,2048]{0,1:T(8,128)(2,1)} %bitcast.186) | data formatting | bytes 4194304 | tf_op jit(solution)/shard_map/dot_general | solution.py:222
  20.0 28.0 %all-gather.3.cloned.1.call-done = bf16[640,2048]{1,0:T(8,128)(2,1)} async-done(((bf16[80,2048]{1,0:T(8,128)(2,1)}), bf16[640,2048]{1,0:T(8,128)(2,1)}) %all-gather.3.cloned.1.call-update) | async-done | bytes 2621456 | tf_op jit(solution)/shard_map/all_gather | solution.py:212
  50.4 2.9 %fusion.76 = f32[512,2,2,128]{0,3,2,1:T(8,128)S(1)} fusion(bf16[512,2048,1,1]{1,0,3,2:T(8,128)(2,1)S(1)} %bitcast.174, bf16[2,2,128,2048]{3,2,1,0:T(8,128)(2,1)} %bitcast.187), kind=kOutput, calls=%fused_computation.153 | convolution fusion | flops 1073741824 | bytes 5242880 | tf_op jit(solution)/shard_map/dot_general | solution.py:222
  54.5 6.4 %reduce-window_add_fusion = s32[8,64,8]{2,0,1:T(8,128)S(1)} fusion(s32[8,64,8]{2,0,1:T(8,128)S(1)} %copy.87), kind=kOutput, calls=%fused_computation.47 | output fusion | flops 262144 | bytes 32768 | tf_op jit(solution)/shard_map/vmap(jit(cumsum))/reduce_window_sum | solution.py:125
  64.9 5.4 %convolution_bitcast_fusion.1 = f32[16,192,128]{2,1,0:T(8,128)S(1)} fusion(bf16[16,2048,128]{2,1,0:T(8,128)(2,1)} %param.26, bf16[192,2048]{1,0:T(8,128)(2,1)} %gather_fusion), kind=kOutput, calls=%fused_computation.32 | convolution fusion | flops 1610612736 | bytes 10747904 | tf_op jit(solution)/shard_map/sd,hdk->hsk/dot_general | solution.py:243
  72.3 3.7 %all-to-all-start = ((bf16[8,2,192,128]{3,2,1,0:T(8,128)(2,1)}), bf16[8,2,192,128]{3,2,1,0:T(8,128)(2,1)S(1)}, u32[]{:S(2)}, u32[]{:S(2)}) async-start(bf16[8,2,192,128]{3,2,1,0:T(8,128)(2,1)} %pad_maximum_fusion), calls=%async_computation | async-start | bytes 1572864 | tf_op jit(solution)/shard_map/all_to_all | solution.py:248
  78.1 3.3 %compare_select_fusion = pred[1536,1536]{0,1:T(8,128)(4,1)} fusion(s32[1536]{0:T(1024)S(1)} %le.27, s32[1536]{0:T(1024)S(1)} %iota_add_fusion, pred[1536]{0:T(1024)(128)(4,1)S(1)} %get-tuple-element.43, pred[1536]{0:T(1024)(128)(4,1)S(1)} %get-tuple-element.44), kind=kLoop, calls=%fused_computation.21 | loop fusion | flops 4718592 | bytes 2374656 | tf_op jit(solution)/shard_map/jit(_where)/select_n | solution.py:157
  81.4 15.3 %all-to-all-done = bf16[8,2,192,128]{3,2,1,0:T(8,128)(2,1)S(1)} async-done(((bf16[8,2,192,128]{3,2,1,0:T(8,128)(2,1)}), bf16[8,2,192,128]{3,2,1,0:T(8,128)(2,1)S(1)}, u32[]{:S(2)}, u32[]{:S(2)}) %all-to-all-start) | async-done | bytes 786464 | tf_op jit(solution)/shard_map/all_to_all | solution.py:248
  97.7 6.2 %fusion.6 = (f32[2,1536]{1,0:T(2,128)S(1)}, f32[2,1536,1536]{1,2,0:T(8,128)S(1)}) fusion(pred[1536,1536]{0,1:T(8,128)(4,1)} %compare_select_fusion, bf16[2,1536,128]{2,1,0:T(8,128)(2,1)} %bitcast.193, bf16[512,2,128]{2,0,1:T(8,128)(2,1)} %copy.96, bf16[1024,2,128]{2,0,1:T(8,128)(2,1)} %bitcast.195), kind=kOutput, calls=%fused_computation.16 | convolution fusion | flops 1223685120 | bytes 22818816 | tf_op jit(solution)/shard_map/hqk,hsk->hqs/dot_general | solution.py:155
  103.9 6.5 %fusion.7 = f32[2,1536]{1,0:T(2,128)S(1)} fusion(f32[2,1536,1536]{1,2,0:T(8,128)S(1)} %get-tuple-element.42, f32[2,1536]{1,0:T(2,128)S(1)} %get-tuple-element.41, pred[1536,1536]{0,1:T(8,128)(4,1)} %compare_select_fusion), kind=kLoop, calls=%fused_computation.17 | loop fusion | flops 18871296 | bytes 21258240 | tf_op jit(solution)/shard_map/reduce_sum | solution.py:163
  111.1 11.1 %fusion.25 = bf16[2,1536,128]{2,1,0:T(8,128)(2,1)S(1)} fusion(f32[2,1536,1536]{1,2,0:T(8,128)} %copy-done.2, f32[2,1536]{1,0:T(2,128)S(1)} %get-tuple-element.41, pred[1536,1536]{0,1:T(8,128)(4,1)} %compare_select_fusion, bf16[512,2,128]{2,0,1:T(8,128)(2,1)} %copy.98, bf16[1024,2,128]{2,0,1:T(8,128)(2,1)} %bitcast.194, f32[2,1536]{1,0:T(2,128)S(1)} %fusion.7), kind=kOutput, calls=%fused_computation.28 | convolution fusion | flops 1229193216 | bytes 22831104 | tf_op jit(solution)/shard_map/hqs,hsk->hqk/dot_general | solution.py:164
  123.2 3.5 %all-to-all-start.1 = ((bf16[8,2,192,128]{3,2,1,0:T(8,128)(2,1)}), bf16[8,2,192,128]{3,2,1,0:T(8,128)(2,1)S(1)}, u32[]{:S(2)}, u32[]{:S(2)}) async-start(bf16[8,2,192,128]{3,2,1,0:T(8,128)(2,1)} %bitcast.167), calls=%async_computation.1 | async-start | bytes 1572864 | tf_op jit(solution)/shard_map/all_to_all | solution.py:259
  129.3 18.3 %all-to-all-done.1 = bf16[8,2,192,128]{3,2,1,0:T(8,128)(2,1)S(1)} async-done(((bf16[8,2,192,128]{3,2,1,0:T(8,128)(2,1)}), bf16[8,2,192,128]{3,2,1,0:T(8,128)(2,1)S(1)}, u32[]{:S(2)}, u32[]{:S(2)}) %all-to-all-start.1) | async-done | bytes 786464 | tf_op jit(solution)/shard_map/all_to_all | solution.py:259
  147.6 5.4 %fusion.18 = bf16[192,2048]{1,0:T(8,128)(2,1)} fusion(bf16[16,192,128]{2,1,0:T(8,128)(2,1)S(1)} %bitcast.190, bf16[16,128,2048]{2,1,0:T(8,128)(2,1)} %param.28), kind=kOutput, calls=%fused_computation.25 | convolution fusion | flops 1611005952 | bytes 9961472 | tf_op jit(solution)/shard_map/hsk,hkd->sd/dot_general | solution.py:261
  153.0 3.7 %all-to-all-start.2 = ((bf16[8,24,2048]{2,1,0:T(8,128)(2,1)}), bf16[8,24,2048]{2,1,0:T(8,128)(2,1)S(1)}, u32[]{:S(2)}, u32[]{:S(2)}) async-start(bf16[8,24,2048]{2,1,0:T(8,128)(2,1)} %bitcast.32), calls=%async_computation.2 | async-start | bytes 1572864 | tf_op jit(solution)/shard_map/all_to_all | solution.py:263
  156.8 20.8 %all-to-all-done.2 = bf16[8,24,2048]{2,1,0:T(8,128)(2,1)S(1)} async-done(((bf16[8,24,2048]{2,1,0:T(8,128)(2,1)}), bf16[8,24,2048]{2,1,0:T(8,128)(2,1)S(1)}, u32[]{:S(2)}, u32[]{:S(2)}) %all-to-all-start.2) | async-done | bytes 786464 | tf_op jit(solution)/shard_map/all_to_all | solution.py:263
  181.6 4.4 %all-to-all-start.3 = ((bf16[8,24,2048]{2,1,0:T(8,128)(2,1)}), bf16[8,24,2048]{2,1,0:T(8,128)(2,1)}, u32[]{:S(2)}, u32[]{:S(2)}) async-start(bf16[8,24,2048]{2,1,0:T(8,128)(2,1)} %bitcast.44), calls=%async_computation.3 | async-start | bytes 1572864 | tf_op jit(solution)/shard_map/all_to_all | solution.py:278
  189.0 4.2 %dynamic_update_slice.3 = bf16[1536,512]{1,0:T(8,128)(2,1)S(1)} dynamic-update-slice(bf16[1536,512]{1,0:T(8,128)(2,1)S(1)} %broadcast_in_dim.47, bf16[512,512]{1,0:T(8,128)(2,1)} %copy.108, s32[]{:T(128)S(6)} %select_n.73, s32[]{:T(128)} %constant.94.clone.1) | dynamic-update-slice | bytes 1048580 | tf_op jit(solution)/shard_map/dynamic_update_slice | solution.py:232
  193.2 13.6 %all-to-all-done.3 = bf16[8,24,2048]{2,1,0:T(8,128)(2,1)} async-done(((bf16[8,24,2048]{2,1,0:T(8,128)(2,1)}), bf16[8,24,2048]{2,1,0:T(8,128)(2,1)}, u32[]{:S(2)}, u32[]{:S(2)}) %all-to-all-start.3) | async-done | bytes 786464 | tf_op jit(solution)/shard_map/all_to_all | solution.py:278
  206.8 14.4 %fusion.4 = f32[192,5632]{1,0:T(8,128)} fusion(bf16[192,2048]{1,0:T(8,128)(2,1)} %bitcast.45, bf16[1,2048,5632]{2,1,0:T(8,128)(2,1)} %param.31), kind=kOutput, calls=%fused_computation.12 | convolution fusion | flops 4429185024 | bytes 28180480 | tf_op jit(solution)/shard_map/dot_general | solution.py:279
  221.2 21.3 %fusion.19 = bf16[192,2048]{1,0:T(8,128)(2,1)} fusion(bf16[1,5632,2048]{2,1,0:T(8,128)(2,1)} %param.33, bf16[192,2048]{1,0:T(8,128)(2,1)} %bitcast.45, bf16[1,2048,5632]{2,1,0:T(8,128)(2,1)} %param.32, f32[192,5632]{1,0:T(8,128)} %fusion.4), kind=kOutput, calls=%fused_computation.26 | convolution fusion | flops 8865251328 | bytes 52035584 | tf_op jit(solution)/shard_map/dot_general | solution.py:282
  242.6 3.7 %all-to-all-start.4 = ((bf16[8,24,2048]{2,1,0:T(8,128)(2,1)}), bf16[8,24,2048]{2,1,0:T(8,128)(2,1)S(1)}, u32[]{:S(2)}, u32[]{:S(2)}) async-start(bf16[8,24,2048]{2,1,0:T(8,128)(2,1)} %bitcast.191), calls=%async_computation.4 | async-start | bytes 1572864 | tf_op jit(solution)/shard_map/all_to_all | solution.py:283
  246.3 2.9 %select_bitcast_fusion = bf16[1,1536,512]{2,1,0:T(8,128)(2,1)} fusion(bf16[1536,512]{1,0:T(8,128)(2,1)S(1)} %dynamic_update_slice.3, bf16[1024,512]{1,0:T(8,128)(2,1)} %bitcast.182, pred[1536]{0:T(1024)(128)(4,1)S(1)} %get-tuple-element.43), kind=kLoop, calls=%fused_computation.29 | loop fusion | flops 786432 | bytes 4195840 | tf_op jit(solution)/shard_map/broadcast_in_dim | solution.py:290
  249.4 17.7 %all-to-all-done.4 = bf16[8,24,2048]{2,1,0:T(8,128)(2,1)S(1)} async-done(((bf16[8,24,2048]{2,1,0:T(8,128)(2,1)}), bf16[8,24,2048]{2,1,0:T(8,128)(2,1)S(1)}, u32[]{:S(2)}, u32[]{:S(2)}) %all-to-all-start.4) | async-done | bytes 786464 | tf_op jit(solution)/shard_map/all_to_all | solution.py:283
  (134 shorter events, 34.4 us)
Async XLA Ops:
  7.2 121.9 %copy-start = (bf16[2048,8]{0,1:T(8,128)(2,1)S(1)}, bf16[2048,8]{0,1:T(8,128)(2,1)}, u32[]{:S(2)}) copy-start(bf16[2048,8]{0,1:T(8,128)(2,1)} %param.25) | copy-start | bytes 98308
  7.2 8.7 %copy-start.6 = (bf16[1,1024,512]{2,1,0:T(8,128)(2,1)S(1)}, bf16[1,1024,512]{2,1,0:T(8,128)(2,1)}, u32[]{:S(2)}) copy-start(bf16[1,1024,512]{2,1,0:T(8,128)(2,1)} %param.20) | copy-start | bytes 3145732
  7.2 40.8 %all-gather.3.cloned.1.call-start = ((), (), s32[]{:S(2)}) async-start(), calls=%async_computation.5 | async-start | bytes 2949120 | tf_op jit(solution)/shard_map/all_gather | solution.py:212
  11.9 6.6 %copy-start.11 = (s32[1,64,2]{1,2,0:T(2,128)S(1)}, s32[1,64,2]{1,2,0:T(2,128)}, u32[]{:S(2)}) copy-start(s32[1,64,2]{1,2,0:T(2,128)} %param.22) | copy-start | bytes 1540
  70.3 5.7 %copy-start.8 = (f32[512,64]{0,1:T(8,128)S(1)}, f32[512,64]{0,1:T(8,128)}, u32[]{:S(2)}) copy-start(f32[512,64]{0,1:T(8,128)} %get-tuple-element.27) | copy-start | bytes 393220
  70.3 5.7 %copy-start.9 = (f32[512,64]{0,1:T(8,128)S(1)}, f32[512,64]{0,1:T(8,128)}, u32[]{:S(2)}) copy-start(f32[512,64]{0,1:T(8,128)} %get-tuple-element.28) | copy-start | bytes 393220
  70.3 5.8 %copy-start.7 = (bf16[512,2,1,128]{0,3,2,1:T(8,128)(2,1)S(1)}, bf16[512,2,1,128]{0,3,2,1:T(8,128)(2,1)}, u32[]{:S(2)}) copy-start(bf16[512,2,1,128]{0,3,2,1:T(8,128)(2,1)} %slice.136) | copy-start | bytes 786436
  72.3 24.5 %all-to-all-start = ((bf16[8,2,192,128]{3,2,1,0:T(8,128)(2,1)}), bf16[8,2,192,128]{3,2,1,0:T(8,128)(2,1)S(1)}, u32[]{:S(2)}, u32[]{:S(2)}) async-start(bf16[8,2,192,128]{3,2,1,0:T(8,128)(2,1)} %pad_maximum_fusion), calls=%async_computation | async-start | bytes 1572864 | tf_op jit(solution)/shard_map/all_to_all | solution.py:248
  76.2 21.4 %copy-start.3 = (bf16[512,2,2,128]{0,3,2,1:T(8,128)(2,1)}, bf16[512,2,2,128]{0,3,2,1:T(8,128)(2,1)S(1)}, u32[]{:S(2)}) copy-start(bf16[512,2,2,128]{0,3,2,1:T(8,128)(2,1)S(1)} %maximum_convert_fusion) | copy-start | bytes 1572868
  103.9 7.2 %copy-start.2 = (f32[2,1536,1536]{1,2,0:T(8,128)}, f32[2,1536,1536]{1,2,0:T(8,128)S(1)}, u32[]{:S(2)}) copy-start(f32[2,1536,1536]{1,2,0:T(8,128)S(1)} %get-tuple-element.42) | copy-start | bytes 56623108
  123.2 24.5 %all-to-all-start.1 = ((bf16[8,2,192,128]{3,2,1,0:T(8,128)(2,1)}), bf16[8,2,192,128]{3,2,1,0:T(8,128)(2,1)S(1)}, u32[]{:S(2)}, u32[]{:S(2)}) async-start(bf16[8,2,192,128]{3,2,1,0:T(8,128)(2,1)} %bitcast.167), calls=%async_computation.1 | async-start | bytes 1572864 | tf_op jit(solution)/shard_map/all_to_all | solution.py:259
  127.0 1.5 copy-start.12
  153.0 26.1 %copy-start.5 = (bf16[1,64,2048]{2,1,0:T(8,128)(2,1)S(1)}, bf16[1,64,2048]{2,1,0:T(8,128)(2,1)}, u32[]{:S(2)}) copy-start(bf16[1,64,2048]{2,1,0:T(8,128)(2,1)} %param.19) | copy-start | bytes 786436
  153.0 26.4 %copy-start.13 = (f32[2048]{0:T(1024)S(1)}, f32[2048]{0:T(1024)}, u32[]{:S(2)}) copy-start(f32[2048]{0:T(1024)} %param.29) | copy-start | bytes 24580
  153.0 24.6 %all-to-all-start.2 = ((bf16[8,24,2048]{2,1,0:T(8,128)(2,1)}), bf16[8,24,2048]{2,1,0:T(8,128)(2,1)S(1)}, u32[]{:S(2)}, u32[]{:S(2)}) async-start(bf16[8,24,2048]{2,1,0:T(8,128)(2,1)} %bitcast.32), calls=%async_computation.2 | async-start | bytes 1572864 | tf_op jit(solution)/shard_map/all_to_all | solution.py:263
  181.6 25.2 %all-to-all-start.3 = ((bf16[8,24,2048]{2,1,0:T(8,128)(2,1)}), bf16[8,24,2048]{2,1,0:T(8,128)(2,1)}, u32[]{:S(2)}, u32[]{:S(2)}) async-start(bf16[8,24,2048]{2,1,0:T(8,128)(2,1)} %bitcast.44), calls=%async_computation.3 | async-start | bytes 1572864 | tf_op jit(solution)/shard_map/all_to_all | solution.py:278
  186.3 1.5 copy-start.4
  242.6 6.6 %copy-start.10 = (bf16[2048,8]{0,1:T(8,128)(2,1)S(1)}, bf16[2048,8]{0,1:T(8,128)(2,1)}, u32[]{:S(2)}) copy-start(bf16[2048,8]{0,1:T(8,128)(2,1)} %param.30) | copy-start | bytes 98308
  242.6 24.6 %all-to-all-start.4 = ((bf16[8,24,2048]{2,1,0:T(8,128)(2,1)}), bf16[8,24,2048]{2,1,0:T(8,128)(2,1)S(1)}, u32[]{:S(2)}, u32[]{:S(2)}) async-start(bf16[8,24,2048]{2,1,0:T(8,128)(2,1)} %bitcast.191), calls=%async_computation.4 | async-start | bytes 1572864 | tf_op jit(solution)/shard_map/all_to_all | solution.py:283
  246.3 23.4 %copy-start.1 = (bf16[2048,8]{0,1:T(8,128)(2,1)S(1)}, bf16[2048,8]{0,1:T(8,128)(2,1)}, u32[]{:S(2)}) copy-start(bf16[2048,8]{0,1:T(8,128)(2,1)} %param.25) | copy-start | bytes 98308
Sparse Core Ops, SparseCore 0:
  11.4 36.5 all-gather.2

commit v2 on v1

--- a/solution.py
+++ b/solution.py
@@ -3,6 +3,8 @@
 import jax
 import jax.numpy as jnp
 from jax import lax
+from jax.experimental import pallas as pl
+from jax.experimental.pallas import tpu as pltpu
 from jax.sharding import PartitionSpec as P
 
 MOST = 24
@@ -119,10 +121,19 @@
     return (running_acc / running_total[:, None]).astype(jnp.bfloat16)
 
 
+def running_count(member):
+    rows = member.shape[0]
+    lower = (
+        jnp.arange(rows, dtype=jnp.int32)[None, :] <= jnp.arange(rows, dtype=jnp.int32)[:, None]
+    ).astype(jnp.bfloat16)
+    counts = jnp.dot(lower, member.astype(jnp.bfloat16), preferred_element_type=jnp.float32)
+    return counts.astype(jnp.int32)
+
+
 def local_slots(routes, labels, slot_count):
     matches = routes[:, :, None] == labels[None, None, :]
     member = jnp.any(matches, axis=1).astype(jnp.int32)
-    ranking = jnp.cumsum(member, axis=0) - 1
+    ranking = running_count(member) - 1
     slot_ids = jnp.arange(slot_count, dtype=jnp.int32)
     onehot = ((member[..., None] > 0) & (ranking[..., None] == slot_ids)).astype(jnp.int32)
     rows = jnp.arange(routes.shape[0], dtype=jnp.int32)[:, None, None]
@@ -132,7 +143,7 @@
 def route_slots(routes, label_count):
     labels = jnp.arange(label_count, dtype=jnp.int32)
     member = jnp.any(routes[:, :, None] == labels[None, None, :], axis=1).astype(jnp.int32)
-    ranking = jnp.cumsum(member, axis=0) - 1
+    ranking = running_count(member) - 1
     return jnp.take_along_axis(ranking, routes, axis=1)
 
 
@@ -148,6 +159,44 @@
             part = part + flat[index].astype(jnp.float32)
         total = total + part * gates[:, route][:, None]
     return total
+
+
+def mlp_kernel(x_ref, gate_ref, up_ref, down_ref, out_ref, acc_ref):
+    step = pl.program_id(0)
+
+    @pl.when(step == 0)
+    def _():
+        acc_ref[...] = jnp.zeros_like(acc_ref)
+
+    rows = x_ref[...]
+    gate_part = jnp.dot(rows, gate_ref[...], preferred_element_type=jnp.float32)
+    up_part = jnp.dot(rows, up_ref[...], preferred_element_type=jnp.float32)
+    hidden = (gate_part / (1.0 + jnp.exp(-gate_part)) * up_part).astype(jnp.bfloat16)
+    acc_ref[...] += jnp.dot(hidden, down_ref[...], preferred_element_type=jnp.float32)
+
+    @pl.when(step == pl.num_programs(0) - 1)
+    def _():
+        out_ref[...] = acc_ref[...].astype(out_ref.dtype)
+
+
+def expert_mlp(rows, w_gate, w_up, w_down):
+    row_count, width = rows.shape
+    hidden_units = w_gate.shape[-1]
+    tile = next(t for t in (512, 256, 128) if hidden_units % t == 0)
+    return pl.pallas_call(
+        mlp_kernel,
+        grid=(hidden_units // tile,),
+        in_specs=[
+            pl.BlockSpec((row_count, width), lambda k: (0, 0)),
+            pl.BlockSpec((None, width, tile), lambda k: (0, 0, k)),
+            pl.BlockSpec((None, width, tile), lambda k: (0, 0, k)),
+            pl.BlockSpec((None, tile, width), lambda k: (0, k, 0)),
+        ],
+        out_specs=pl.BlockSpec((row_count, width), lambda k: (0, 0)),
+        out_shape=jax.ShapeDtypeStruct((row_count, width), jnp.bfloat16),
+        scratch_shapes=[pltpu.VMEM((row_count, width), jnp.float32)],
+        compiler_params=pltpu.CompilerParams(dimension_semantics=("arbitrary",)),
+    )(rows, w_gate, w_up, w_down)
 
 
 def head_attention(queries, query_pos, keys, values, length, cache_limit):
@@ -276,10 +325,7 @@
     dest_tokens = jnp.repeat(mlp_tokens, split_count, axis=0)
     send_m = normed_mlp[dest_tokens.reshape(-1)].reshape(device_count, slot_count, model_width)
     inputs = lax.all_to_all(send_m, "exp", 0, 0, tiled=True).reshape(-1, model_width)
-    gate_part = jnp.dot(inputs, w_gate[0], preferred_element_type=jnp.float32)
-    up_part = jnp.dot(inputs, w_up[0], preferred_element_type=jnp.float32)
-    hidden = (jax.nn.silu(gate_part) * up_part).astype(jnp.bfloat16)
-    slice_out = jnp.dot(hidden, w_down[0], preferred_element_type=jnp.float32).astype(jnp.bfloat16)
+    slice_out = expert_mlp(inputs, w_gate, w_up, w_down)
     recv_m = lax.all_to_all(
         slice_out.reshape(device_count, slot_count, model_width), "exp", 0, 0, tiled=True
     )

time: 278 us -> 263 us (0.946)
  matrix products: 67.2 us -> 31.9 us
  Pallas kernels: 0 us -> 28.6 us
  other arithmetic: 30.1 us -> 23.4 us
    dot_general x2, matrix products: 35.8 us -> 0.26 us  [running_count(): jnp.dot(lower, member.astype(jnp.bfloat16), preferred_element_type=jnp.fl...]
    pallas_call x0 -> x1, Pallas kernels: none -> 28.6 us  [expert_mlp(): pl.pallas_call(mlp_kernel, grid=(hidden_units // tile,), in_specs=[pl.Blo...]
    another operation x4 -> x1, other arithmetic: 7.17 us -> 0.62 us  [the longest x2 6.46 us: local_slots(): ranking = jnp.cumsum(member, axis=0) - 1]
  transfers between devices with their start and end apart: 6 -> 6, of which waited for: 6 -> 6; matrix products, arithmetic and copies ran while one was open for 9% -> 10% of each run, Pallas kernels for 0% -> 0%
where the time goes in v2:
time: 263 us; the launch traced here: 262 us
  waiting for transfers between devices  114 us (43%)
  matrix products  31.9 us (12%)
  local copies, waits for them, and re-layouts  29.9 us (11%)
  Pallas kernels  28.6 us (11%)
  other arithmetic  23.4 us (9%)
  starting transfers between devices  19 us (7%)
  between operations  15.3 us (6%)
    pallas_call x1, Pallas kernels, expert_mlp(): pl.pallas_call(mlp_kernel, grid=(hidden_units // tile,), in_specs=[pl.Blo...  28.6 us
    all_gather x1, waiting for transfers between devices, body(): lax.all_gather(jnp.concatenate([normed, route_rows], axis=0), 'exp', axis...  28.2 us
    all_to_all x1, waiting for transfers between devices, body(): recv_p = lax.all_to_all(send_p, 'exp', 0, 0, tiled=True)  20.8 us
    all_to_all x1, waiting for transfers between devices, body(): recv_o = lax.all_to_all(send_o, 'exp', 0, 0, tiled=True)  18.5 us
    all_to_all x1, waiting for transfers between devices, body(): lax.all_to_all(slice_out.reshape(device_count, slot_count, model_width),...  17.7 us
    all_to_all x1, waiting for transfers between devices, body(): recv_q = lax.all_to_all(send_q, 'exp', 0, 0, tiled=True)  15.4 us
    all_to_all x1, waiting for transfers between devices, body(): lax.all_to_all(send_m, 'exp', 0, 0, tiled=True).reshape(-1, model_width)  13.9 us
    dot_general x1, matrix products, head_attention(): jnp.einsum('hqs,hsk->hqk', weights.astype(jnp.bfloat16), values, preferre...  11.1 us
  transfers between devices with their start and end apart: 6, of which 6 were waited for; matrix products, arithmetic and copies ran while one was open for 10% of the time, Pallas kernels for 0%

profile of v2, /device:TPU:0, one launch (start us, length us, event | category | flops | bytes accessed | tf_op | source)
XLA Modules:
  0.0 262.5 jit_solution(2926452313912118630)
XLA Ops:
  11.9 4.0 %copy.109 = bf16[512,2048]{1,0:T(8,128)(2,1)} copy(bf16[512,2048]{0,1:T(8,128)(2,1)} %bitcast.182) | data formatting | bytes 4194304 | tf_op jit(solution)/shard_map/dot_general | solution.py:271
  19.7 28.2 %all-gather.3.cloned.1.call-done = bf16[640,2048]{1,0:T(8,128)(2,1)} async-done(((bf16[80,2048]{1,0:T(8,128)(2,1)}), bf16[640,2048]{1,0:T(8,128)(2,1)}) %all-gather.3.cloned.1.call-update) | async-done | bytes 2621456 | tf_op jit(solution)/shard_map/all_gather | solution.py:261
  50.8 2.9 %fusion.65 = f32[512,2,2,128]{0,3,2,1:T(8,128)S(1)} fusion(bf16[512,2048,1,1]{1,0,3,2:T(8,128)(2,1)S(1)} %bitcast.169, bf16[2,2,128,2048]{3,2,1,0:T(8,128)(2,1)} %bitcast.183), kind=kOutput, calls=%fused_computation.153 | convolution fusion | flops 1073741824 | bytes 5242880 | tf_op jit(solution)/shard_map/dot_general | solution.py:271
  56.0 2.0 gather_fusion
  58.1 5.4 %convolution_bitcast_fusion.1 = f32[16,192,128]{2,1,0:T(8,128)S(1)} fusion(bf16[16,2048,128]{2,1,0:T(8,128)(2,1)} %param.26, bf16[192,2048]{1,0:T(8,128)(2,1)} %gather_fusion), kind=kOutput, calls=%fused_computation.23 | convolution fusion | flops 1610612736 | bytes 10747904 | tf_op jit(solution)/shard_map/sd,hdk->hsk/dot_general | solution.py:292
  65.5 3.9 %all-to-all-start = ((bf16[8,2,192,128]{3,2,1,0:T(8,128)(2,1)}), bf16[8,2,192,128]{3,2,1,0:T(8,128)(2,1)S(1)}, u32[]{:S(2)}, u32[]{:S(2)}) async-start(bf16[8,2,192,128]{3,2,1,0:T(8,128)(2,1)} %pad_maximum_fusion), calls=%async_computation | async-start | bytes 1572864 | tf_op jit(solution)/shard_map/all_to_all | solution.py:297
  71.4 3.3 %compare_select_fusion = pred[1536,1536]{0,1:T(8,128)(4,1)} fusion(s32[1536]{0:T(1024)S(1)} %le.76, s32[1536]{0:T(1024)S(1)} %iota_add_fusion, pred[1536]{0:T(1024)(128)(4,1)S(1)} %get-tuple-element.39, pred[1536]{0:T(1024)(128)(4,1)S(1)} %get-tuple-element.40), kind=kLoop, calls=%fused_computation.15 | loop fusion | flops 4718592 | bytes 2374656 | tf_op jit(solution)/shard_map/jit(_where)/select_n | solution.py:206
  74.7 15.4 %all-to-all-done = bf16[8,2,192,128]{3,2,1,0:T(8,128)(2,1)S(1)} async-done(((bf16[8,2,192,128]{3,2,1,0:T(8,128)(2,1)}), bf16[8,2,192,128]{3,2,1,0:T(8,128)(2,1)S(1)}, u32[]{:S(2)}, u32[]{:S(2)}) %all-to-all-start) | async-done | bytes 786464 | tf_op jit(solution)/shard_map/all_to_all | solution.py:297
  91.0 6.2 %fusion = (f32[2,1536]{1,0:T(2,128)S(1)}, f32[2,1536,1536]{1,2,0:T(8,128)S(1)}) fusion(pred[1536,1536]{0,1:T(8,128)(4,1)} %compare_select_fusion, bf16[2,1536,128]{2,1,0:T(8,128)(2,1)} %bitcast.188, bf16[512,2,128]{2,0,1:T(8,128)(2,1)} %copy.97, bf16[1024,2,128]{2,0,1:T(8,128)(2,1)} %bitcast.190), kind=kOutput, calls=%fused_computation.10 | convolution fusion | flops 1223685120 | bytes 22818816 | tf_op jit(solution)/shard_map/hqk,hsk->hqs/dot_general | solution.py:204
  97.2 6.5 %fusion.1 = f32[2,1536]{1,0:T(2,128)S(1)} fusion(f32[2,1536,1536]{1,2,0:T(8,128)S(1)} %get-tuple-element.38, f32[2,1536]{1,0:T(2,128)S(1)} %get-tuple-element.37, pred[1536,1536]{0,1:T(8,128)(4,1)} %compare_select_fusion), kind=kLoop, calls=%fused_computation.11 | loop fusion | flops 18871296 | bytes 21258240 | tf_op jit(solution)/shard_map/reduce_sum | solution.py:212
  104.4 11.1 %fusion.10 = bf16[2,1536,128]{2,1,0:T(8,128)(2,1)S(1)} fusion(f32[2,1536,1536]{1,2,0:T(8,128)} %copy-done.2, f32[2,1536]{1,0:T(2,128)S(1)} %get-tuple-element.37, pred[1536,1536]{0,1:T(8,128)(4,1)} %compare_select_fusion, bf16[512,2,128]{2,0,1:T(8,128)(2,1)} %copy.99, bf16[1024,2,128]{2,0,1:T(8,128)(2,1)} %bitcast.189, f32[2,1536]{1,0:T(2,128)S(1)} %fusion.1), kind=kOutput, calls=%fused_computation.19 | convolution fusion | flops 1229193216 | bytes 22831104 | tf_op jit(solution)/shard_map/hqs,hsk->hqk/dot_general | solution.py:213
  116.5 3.5 %all-to-all-start.1 = ((bf16[8,2,192,128]{3,2,1,0:T(8,128)(2,1)}), bf16[8,2,192,128]{3,2,1,0:T(8,128)(2,1)S(1)}, u32[]{:S(2)}, u32[]{:S(2)}) async-start(bf16[8,2,192,128]{3,2,1,0:T(8,128)(2,1)} %bitcast.162), calls=%async_computation.1 | async-start | bytes 1572864 | tf_op jit(solution)/shard_map/all_to_all | solution.py:308
  122.4 18.5 %all-to-all-done.1 = bf16[8,2,192,128]{3,2,1,0:T(8,128)(2,1)S(1)} async-done(((bf16[8,2,192,128]{3,2,1,0:T(8,128)(2,1)}), bf16[8,2,192,128]{3,2,1,0:T(8,128)(2,1)S(1)}, u32[]{:S(2)}, u32[]{:S(2)}) %all-to-all-start.1) | async-done | bytes 786464 | tf_op jit(solution)/shard_map/all_to_all | solution.py:308
  140.9 5.5 %fusion.6 = bf16[192,2048]{1,0:T(8,128)(2,1)} fusion(bf16[16,192,128]{2,1,0:T(8,128)(2,1)S(1)} %bitcast.186, bf16[16,128,2048]{2,1,0:T(8,128)(2,1)} %param.28), kind=kOutput, calls=%fused_computation.17 | convolution fusion | flops 1611005952 | bytes 9961472 | tf_op jit(solution)/shard_map/hsk,hkd->sd/dot_general | solution.py:310
  146.4 3.5 %all-to-all-start.2 = ((bf16[8,24,2048]{2,1,0:T(8,128)(2,1)}), bf16[8,24,2048]{2,1,0:T(8,128)(2,1)S(1)}, u32[]{:S(2)}, u32[]{:S(2)}) async-start(bf16[8,24,2048]{2,1,0:T(8,128)(2,1)} %bitcast.36), calls=%async_computation.2 | async-start | bytes 1572864 | tf_op jit(solution)/shard_map/all_to_all | solution.py:312
  150.1 20.8 %all-to-all-done.2 = bf16[8,24,2048]{2,1,0:T(8,128)(2,1)S(1)} async-done(((bf16[8,24,2048]{2,1,0:T(8,128)(2,1)}), bf16[8,24,2048]{2,1,0:T(8,128)(2,1)S(1)}, u32[]{:S(2)}, u32[]{:S(2)}) %all-to-all-start.2) | async-done | bytes 786464 | tf_op jit(solution)/shard_map/all_to_all | solution.py:312
  172.8 2.0 gather_fusion.3
  174.9 4.4 %all-to-all-start.3 = ((bf16[8,24,2048]{2,1,0:T(8,128)(2,1)}), bf16[8,24,2048]{2,1,0:T(8,128)(2,1)}, u32[]{:S(2)}, u32[]{:S(2)}) async-start(bf16[8,24,2048]{2,1,0:T(8,128)(2,1)} %bitcast.48), calls=%async_computation.3 | async-start | bytes 1572864 | tf_op jit(solution)/shard_map/all_to_all | solution.py:327
  182.0 4.2 %dynamic_update_slice.3 = bf16[1536,512]{1,0:T(8,128)(2,1)S(1)} dynamic-update-slice(bf16[1536,512]{1,0:T(8,128)(2,1)S(1)} %broadcast_in_dim.43, bf16[512,512]{1,0:T(8,128)(2,1)} %copy.106, s32[]{:T(128)S(6)} %select_n.73, s32[]{:T(128)} %constant.84.clone.1) | dynamic-update-slice | bytes 1048580 | tf_op jit(solution)/shard_map/dynamic_update_slice | solution.py:281
  186.2 13.9 %all-to-all-done.3 = bf16[8,24,2048]{2,1,0:T(8,128)(2,1)} async-done(((bf16[8,24,2048]{2,1,0:T(8,128)(2,1)}), bf16[8,24,2048]{2,1,0:T(8,128)(2,1)}, u32[]{:S(2)}, u32[]{:S(2)}) %all-to-all-start.3) | async-done | bytes 786464 | tf_op jit(solution)/shard_map/all_to_all | solution.py:327
  200.0 28.6 %shard_map.158 = bf16[192,2048]{1,0:T(8,128)(2,1)} custom-call(bf16[192,2048]{1,0:T(8,128)(2,1)} %bitcast.49.x_ref, bf16[1,2048,5632]{2,1,0:T(8,128)(2,1)} %gate_ref.1, bf16[1,2048,5632]{2,1,0:T(8,128)(2,1)} %up_ref.1, bf16[1,5632,2048]{2,1,0:T(8,128)(2,1)} %down_ref.1), custom_call_target="tpu_custom_call" | custom-call | tf_op jit(solution)/shard_map/pallas_call | solution.py:186
  228.7 3.5 %all-to-all-start.4 = ((bf16[8,24,2048]{2,1,0:T(8,128)(2,1)}), bf16[8,24,2048]{2,1,0:T(8,128)(2,1)S(1)}, u32[]{:S(2)}, u32[]{:S(2)}) async-start(bf16[8,24,2048]{2,1,0:T(8,128)(2,1)} %bitcast.178), calls=%async_computation.4 | async-start | bytes 1572864 | tf_op jit(solution)/shard_map/all_to_all | solution.py:329
  232.2 2.9 %select_bitcast_fusion = bf16[1,1536,512]{2,1,0:T(8,128)(2,1)} fusion(bf16[1536,512]{1,0:T(8,128)(2,1)S(1)} %dynamic_update_slice.3, bf16[1024,512]{1,0:T(8,128)(2,1)} %bitcast.177, pred[1536]{0:T(1024)(128)(4,1)S(1)} %get-tuple-element.39), kind=kLoop, calls=%fused_computation.20 | loop fusion | flops 786432 | bytes 4195840 | tf_op jit(solution)/shard_map/broadcast_in_dim | solution.py:336
  235.4 17.7 %all-to-all-done.4 = bf16[8,24,2048]{2,1,0:T(8,128)(2,1)S(1)} async-done(((bf16[8,24,2048]{2,1,0:T(8,128)(2,1)}), bf16[8,24,2048]{2,1,0:T(8,128)(2,1)S(1)}, u32[]{:S(2)}, u32[]{:S(2)}) %all-to-all-start.4) | async-done | bytes 786464 | tf_op jit(solution)/shard_map/all_to_all | solution.py:329
  (125 shorter events, 29.2 us)
Async XLA Ops:
  7.2 115.0 %copy-start = (bf16[2048,8]{0,1:T(8,128)(2,1)S(1)}, bf16[2048,8]{0,1:T(8,128)(2,1)}, u32[]{:S(2)}) copy-start(bf16[2048,8]{0,1:T(8,128)(2,1)} %param.25) | copy-start | bytes 98308
  7.2 40.7 %all-gather.3.cloned.1.call-start = ((), (), s32[]{:S(2)}) async-start(), calls=%async_computation.5 | async-start | bytes 2949120 | tf_op jit(solution)/shard_map/all_gather | solution.py:261
  11.1 4.7 %copy-start.6 = (bf16[1,1024,512]{2,1,0:T(8,128)(2,1)S(1)}, bf16[1,1024,512]{2,1,0:T(8,128)(2,1)}, u32[]{:S(2)}) copy-start(bf16[1,1024,512]{2,1,0:T(8,128)(2,1)} %param.20) | copy-start | bytes 3145732
  55.0 0.6 copy-start.8
  64.1 5.2 %copy-start.7 = (f32[512,64]{0,1:T(8,128)S(1)}, f32[512,64]{0,1:T(8,128)}, u32[]{:S(2)}) copy-start(f32[512,64]{0,1:T(8,128)} %get-tuple-element.26) | copy-start | bytes 393220
  65.5 4.1 %copy-start.9 = (s32[8,8,24]{2,1,0:T(8,128)S(1)}, s32[8,8,24]{2,1,0:T(8,128)}, u32[]{:S(2)}) copy-start(s32[8,8,24]{2,1,0:T(8,128)} %copy-done.8) | copy-start | bytes 18436
  65.5 24.6 %all-to-all-start = ((bf16[8,2,192,128]{3,2,1,0:T(8,128)(2,1)}), bf16[8,2,192,128]{3,2,1,0:T(8,128)(2,1)S(1)}, u32[]{:S(2)}, u32[]{:S(2)}) async-start(bf16[8,2,192,128]{3,2,1,0:T(8,128)(2,1)} %pad_maximum_fusion), calls=%async_computation | async-start | bytes 1572864 | tf_op jit(solution)/shard_map/all_to_all | solution.py:297
  69.5 21.4 %copy-start.3 = (bf16[512,2,2,128]{0,3,2,1:T(8,128)(2,1)}, bf16[512,2,2,128]{0,3,2,1:T(8,128)(2,1)S(1)}, u32[]{:S(2)}) copy-start(bf16[512,2,2,128]{0,3,2,1:T(8,128)(2,1)S(1)} %maximum_convert_fusion) | copy-start | bytes 1572868
  97.2 7.2 %copy-start.2 = (f32[2,1536,1536]{1,2,0:T(8,128)}, f32[2,1536,1536]{1,2,0:T(8,128)S(1)}, u32[]{:S(2)}) copy-start(f32[2,1536,1536]{1,2,0:T(8,128)S(1)} %get-tuple-element.38) | copy-start | bytes 56623108
  115.5 4.5 %copy-start.11 = (s32[1,64,2]{1,2,0:T(2,128)S(1)}, s32[1,64,2]{1,2,0:T(2,128)}, u32[]{:S(2)}) copy-start(s32[1,64,2]{1,2,0:T(2,128)} %param.22) | copy-start | bytes 1540
  116.5 24.5 %all-to-all-start.1 = ((bf16[8,2,192,128]{3,2,1,0:T(8,128)(2,1)}), bf16[8,2,192,128]{3,2,1,0:T(8,128)(2,1)S(1)}, u32[]{:S(2)}, u32[]{:S(2)}) async-start(bf16[8,2,192,128]{3,2,1,0:T(8,128)(2,1)} %bitcast.162), calls=%async_computation.1 | async-start | bytes 1572864 | tf_op jit(solution)/shard_map/all_to_all | solution.py:308
  120.4 1.2 copy-start.12
  146.4 24.5 %all-to-all-start.2 = ((bf16[8,24,2048]{2,1,0:T(8,128)(2,1)}), bf16[8,24,2048]{2,1,0:T(8,128)(2,1)S(1)}, u32[]{:S(2)}, u32[]{:S(2)}) async-start(bf16[8,24,2048]{2,1,0:T(8,128)(2,1)} %bitcast.36), calls=%async_computation.2 | async-start | bytes 1572864 | tf_op jit(solution)/shard_map/all_to_all | solution.py:312
  170.8 1.5 copy-start.5
  170.8 1.8 copy-start.13
  174.9 25.2 %all-to-all-start.3 = ((bf16[8,24,2048]{2,1,0:T(8,128)(2,1)}), bf16[8,24,2048]{2,1,0:T(8,128)(2,1)}, u32[]{:S(2)}, u32[]{:S(2)}) async-start(bf16[8,24,2048]{2,1,0:T(8,128)(2,1)} %bitcast.48), calls=%async_computation.3 | async-start | bytes 1572864 | tf_op jit(solution)/shard_map/all_to_all | solution.py:327
  179.5 1.3 copy-start.4
  228.7 24.4 %all-to-all-start.4 = ((bf16[8,24,2048]{2,1,0:T(8,128)(2,1)}), bf16[8,24,2048]{2,1,0:T(8,128)(2,1)S(1)}, u32[]{:S(2)}, u32[]{:S(2)}) async-start(bf16[8,24,2048]{2,1,0:T(8,128)(2,1)} %bitcast.178), calls=%async_computation.4 | async-start | bytes 1572864 | tf_op jit(solution)/shard_map/all_to_all | solution.py:329
  232.2 2.9 %copy-start.10 = (bf16[2048,8]{0,1:T(8,128)(2,1)S(1)}, bf16[2048,8]{0,1:T(8,128)(2,1)}, u32[]{:S(2)}) copy-start(bf16[2048,8]{0,1:T(8,128)(2,1)} %param.30) | copy-start | bytes 98308
  253.1 2.5 copy-start.1
Sparse Core Ops, SparseCore 0:
  11.3 36.5 all-gather.2

commit v3 on v2

--- a/solution.py
+++ b/solution.py
@@ -1,3 +1,4 @@
+import functools
 import math
 
 import jax
@@ -197,6 +198,52 @@
         scratch_shapes=[pltpu.VMEM((row_count, width), jnp.float32)],
         compiler_params=pltpu.CompilerParams(dimension_semantics=("arbitrary",)),
     )(rows, w_gate, w_up, w_down)
+
+
+def attention_kernel(length_ref, query_ref, pos_ref, key_ref, value_ref, out_ref, *, cache_limit):
+    length = length_ref[0]
+    queries = query_ref[...]
+    factor = queries.shape[-1] ** (-0.5)
+    scores = (
+        lax.dot_general(
+            queries, key_ref[...], (((1,), (1,)), ((), ())), preferred_element_type=jnp.float32
+        )
+        * factor
+    )
+    column = lax.broadcasted_iota(jnp.int32, scores.shape, 1)
+    in_cache = column < cache_limit
+    visible = (in_cache & (column < length)) | (
+        jnp.logical_not(in_cache) & (column - cache_limit <= pos_ref[...])
+    )
+    scores = jnp.where(visible, scores, masked_score)
+    top = jnp.max(scores, axis=1, keepdims=True)
+    weights = jnp.exp(scores - top)
+    total = jnp.sum(weights, axis=1, keepdims=True)
+    summed = jnp.dot(weights.astype(jnp.bfloat16), value_ref[...], preferred_element_type=jnp.float32)
+    out_ref[...] = (summed / total).astype(out_ref.dtype)
+
+
+def kernel_attention(queries, query_pos, keys, values, length, cache_limit):
+    head_count, query_count, head_dim = queries.shape
+    key_count = keys.shape[1]
+    tile = next(t for t in (256, 128, 64, 32, 16, 8) if query_count % t == 0)
+    grid_spec = pltpu.PrefetchScalarGridSpec(
+        num_scalar_prefetch=1,
+        grid=(head_count, query_count // tile),
+        in_specs=[
+            pl.BlockSpec((None, tile, head_dim), lambda h, i, n: (h, i, 0)),
+            pl.BlockSpec((tile, 1), lambda h, i, n: (i, 0)),
+            pl.BlockSpec((None, key_count, head_dim), lambda h, i, n: (h, 0, 0)),
+            pl.BlockSpec((None, key_count, head_dim), lambda h, i, n: (h, 0, 0)),
+        ],
+        out_specs=pl.BlockSpec((None, tile, head_dim), lambda h, i, n: (h, i, 0)),
+    )
+    return pl.pallas_call(
+        functools.partial(attention_kernel, cache_limit=cache_limit),
+        grid_spec=grid_spec,
+        out_shape=jax.ShapeDtypeStruct(queries.shape, jnp.bfloat16),
+        compiler_params=pltpu.CompilerParams(dimension_semantics=("arbitrary", "arbitrary")),
+    )(jnp.reshape(length, (1,)).astype(jnp.int32), queries, query_pos.reshape(-1, 1), keys, values)
 
 
 def head_attention(queries, query_pos, keys, values, length, cache_limit):
@@ -301,7 +348,7 @@
     split_fresh = fresh_kv.reshape(row_total, heads_local, 2, head_dim)
     keys = jnp.swapaxes(jnp.concatenate([split_old[:, :, 0], split_fresh[:, :, 0]], axis=0), 0, 1)
     values = jnp.swapaxes(jnp.concatenate([split_old[:, :, 1], split_fresh[:, :, 1]], axis=0), 0, 1)
-    head_outs = head_attention(recv_q, query_pos, keys, values, length, cache_limit)
+    head_outs = kernel_attention(recv_q, query_pos, keys, values, length, cache_limit)
     send_o = jnp.swapaxes(
         head_outs.reshape(heads_local, device_count, query_slots, head_dim), 0, 1
     )

time: 263 us -> 251 us (0.954)
  matrix products: 31.9 us -> 15.3 us
  Pallas kernels: 28.6 us -> 42.4 us
  other arithmetic: 23.4 us -> 16.4 us
    dot_general x2 -> x0, matrix products: 17.3 us -> none  [the longest x1 11.1 us: head_attention(): jnp.einsum('hqs,hsk->hqk', weights.astype(jnp.bfloat16), values, preferre...]
    pallas_call x0 -> x1, Pallas kernels: none -> 13.8 us  [kernel_attention(): pl.pallas_call(functools.partial(attention_kernel, cache_limit=cache_limi...]
    reduce_sum x1 -> x0, other arithmetic: 6.51 us -> none  [head_attention(): total = jnp.sum(weights, axis=-1, keepdims=True)]
    all_to_all x1, waiting for transfers between devices: 15.4 us -> 12 us  [body(): recv_q = lax.all_to_all(send_q, 'exp', 0, 0, tiled=True)]
    select_n x1 -> x0, other arithmetic: 3.32 us -> none  [head_attention(): jnp.where(slot_ids < cache_limit, slot_ids < length, slot_ids - cache_lim...]
  transfers between devices with their start and end apart: 6 -> 6, of which waited for: 6 -> 6; matrix products, arithmetic and copies ran while one was open for 10% -> 11% of each run, Pallas kernels for 0% -> 0%
where the time goes in v3:
time: 251 us; the launch traced here: 250 us
  waiting for transfers between devices  112 us (45%)
  Pallas kernels  42.4 us (17%)
  local copies, waits for them, and re-layouts  30.2 us (12%)
  starting transfers between devices  18 us (7%)
  other arithmetic  16.4 us (7%)
  matrix products  15.3 us (6%)
  between operations  15.3 us (6%)
    pallas_call x1, Pallas kernels, expert_mlp(): pl.pallas_call(mlp_kernel, grid=(hidden_units // tile,), in_specs=[pl.Blo...  28.6 us
    all_gather x1, waiting for transfers between devices, body(): lax.all_gather(jnp.concatenate([normed, route_rows], axis=0), 'exp', axis...  27.6 us
    all_to_all x1, waiting for transfers between devices, body(): recv_p = lax.all_to_all(send_p, 'exp', 0, 0, tiled=True)  20.8 us
    all_to_all x1, waiting for transfers between devices, body(): recv_o = lax.all_to_all(send_o, 'exp', 0, 0, tiled=True)  18.4 us
    all_to_all x1, waiting for transfers between devices, body(): lax.all_to_all(slice_out.reshape(device_count, slot_count, model_width),...  17.7 us
    all_to_all x1, waiting for transfers between devices, body(): lax.all_to_all(send_m, 'exp', 0, 0, tiled=True).reshape(-1, model_width)  15.7 us
    pallas_call x1, Pallas kernels, kernel_attention(): pl.pallas_call(functools.partial(attention_kernel, cache_limit=cache_limi...  13.8 us
    all_to_all x1, waiting for transfers between devices, body(): recv_q = lax.all_to_all(send_q, 'exp', 0, 0, tiled=True)  12 us
  transfers between devices with their start and end apart: 6, of which 6 were waited for; matrix products, arithmetic and copies ran while one was open for 11% of the time, Pallas kernels for 0%

profile of v3, /device:TPU:0, one launch (start us, length us, event | category | flops | bytes accessed | tf_op | source)
XLA Modules:
  0.0 249.6 jit_solution(17729739856465219607)
XLA Ops:
  11.8 4.0 %copy.127 = bf16[512,2048]{1,0:T(8,128)(2,1)} copy(bf16[512,2048]{0,1:T(8,128)(2,1)} %bitcast.174) | data formatting | bytes 4194304 | tf_op jit(solution)/shard_map/dot_general | solution.py:318
  18.5 1.8 multiply_cosine_fusion
  20.3 27.6 %all-gather.3.cloned.1.call-done = bf16[640,2048]{1,0:T(8,128)(2,1)} async-done(((bf16[80,2048]{1,0:T(8,128)(2,1)}), bf16[640,2048]{1,0:T(8,128)(2,1)}) %all-gather.3.cloned.1.call-update) | async-done | bytes 2621456 | tf_op jit(solution)/shard_map/all_gather | solution.py:308
  49.0 1.7 slice.128
  54.4 5.2 %convolution_bitcast_fusion.1 = f32[16,192,128]{2,1,0:T(8,128)S(1)} fusion(bf16[16,2048,128]{2,1,0:T(8,128)(2,1)} %param.26, bf16[192,2048]{1,0:T(8,128)(2,1)S(1)} %gather_fusion), kind=kOutput, calls=%fused_computation.15 | convolution fusion | flops 1610612736 | bytes 10747904 | tf_op jit(solution)/shard_map/sd,hdk->hsk/dot_general | solution.py:339
  60.3 1.3 pad_maximum_fusion
  61.6 3.5 %all-to-all-start = ((bf16[8,2,192,128]{3,2,1,0:T(8,128)(2,1)}), bf16[8,2,192,128]{3,2,1,0:T(8,128)(2,1)S(1)}, u32[]{:S(2)}, u32[]{:S(2)}) async-start(bf16[8,2,192,128]{3,2,1,0:T(8,128)(2,1)} %pad_maximum_fusion), calls=%async_computation | async-start | bytes 1572864 | tf_op jit(solution)/shard_map/all_to_all | solution.py:344
  65.1 3.8 %fusion.1 = f32[512,2,2,128]{3,0,1,2:T(8,128)} fusion(bf16[512,2048,1,1]{1,0,2,3:T(8,128)(2,1)S(1)} %bitcast.160, bf16[2,2,128,2048]{3,2,1,0:T(8,128)(2,1)} %bitcast.175), kind=kOutput, calls=%fused_computation.10 | convolution fusion | flops 1073741824 | bytes 5242880 | tf_op jit(solution)/shard_map/dot_general | solution.py:318
  74.0 12.0 %all-to-all-done = bf16[8,2,192,128]{3,2,1,0:T(8,128)(2,1)S(1)} async-done(((bf16[8,2,192,128]{3,2,1,0:T(8,128)(2,1)}), bf16[8,2,192,128]{3,2,1,0:T(8,128)(2,1)S(1)}, u32[]{:S(2)}, u32[]{:S(2)}) %all-to-all-start) | async-done | bytes 786464 | tf_op jit(solution)/shard_map/all_to_all | solution.py:344
  87.0 13.8 %shard_map.158 = bf16[2,1536,128]{2,1,0:T(8,128)(2,1)} custom-call(s32[1]{0:T(128)} %copy.136.length_ref, bf16[2,1536,128]{2,1,0:T(8,128)(2,1)} %bitcast.172, s32[1536,1]{1,0:T(8,128)} %reshape_reshape_reshape.4.pos_ref, bf16[2,1536,128]{2,1,0:T(8,128)(2,1)} %get-tuple-element.37.key_ref, bf16[2,1536,128]{2,1,0:T(8,128)(2,1)} %get-tuple-element.38.value_ref), custom_call_target="tpu_custom_call" | custom-call | tf_op jit(solution)/shard_map/pallas_call | solution.py:241
  100.7 2.1 copy.134
  102.8 3.7 %all-to-all-start.1 = ((bf16[8,2,192,128]{3,2,1,0:T(8,128)(2,1)}), bf16[8,2,192,128]{3,2,1,0:T(8,128)(2,1)S(1)}, u32[]{:S(2)}, u32[]{:S(2)}) async-start(bf16[8,2,192,128]{3,2,1,0:T(8,128)(2,1)} %bitcast.152), calls=%async_computation.1 | async-start | bytes 1572864 | tf_op jit(solution)/shard_map/all_to_all | solution.py:355
  108.9 18.4 %all-to-all-done.1 = bf16[8,2,192,128]{3,2,1,0:T(8,128)(2,1)S(1)} async-done(((bf16[8,2,192,128]{3,2,1,0:T(8,128)(2,1)}), bf16[8,2,192,128]{3,2,1,0:T(8,128)(2,1)S(1)}, u32[]{:S(2)}, u32[]{:S(2)}) %all-to-all-start.1) | async-done | bytes 786464 | tf_op jit(solution)/shard_map/all_to_all | solution.py:355
  127.3 5.5 %fusion = bf16[192,2048]{1,0:T(8,128)(2,1)} fusion(bf16[16,192,128]{2,1,0:T(8,128)(2,1)S(1)} %bitcast.181, bf16[16,128,2048]{2,1,0:T(8,128)(2,1)} %param.28), kind=kOutput, calls=%fused_computation.9 | convolution fusion | flops 1611005952 | bytes 9961472 | tf_op jit(solution)/shard_map/hsk,hkd->sd/dot_general | solution.py:357
  132.8 3.5 %all-to-all-start.2 = ((bf16[8,24,2048]{2,1,0:T(8,128)(2,1)}), bf16[8,24,2048]{2,1,0:T(8,128)(2,1)S(1)}, u32[]{:S(2)}, u32[]{:S(2)}) async-start(bf16[8,24,2048]{2,1,0:T(8,128)(2,1)} %bitcast.35), calls=%async_computation.2 | async-start | bytes 1572864 | tf_op jit(solution)/shard_map/all_to_all | solution.py:359
  136.4 20.8 %all-to-all-done.2 = bf16[8,24,2048]{2,1,0:T(8,128)(2,1)S(1)} async-done(((bf16[8,24,2048]{2,1,0:T(8,128)(2,1)}), bf16[8,24,2048]{2,1,0:T(8,128)(2,1)S(1)}, u32[]{:S(2)}, u32[]{:S(2)}) %all-to-all-start.2) | async-done | bytes 786464 | tf_op jit(solution)/shard_map/all_to_all | solution.py:359
  159.5 2.0 gather_fusion.3
  161.5 3.5 %all-to-all-start.3 = ((bf16[8,24,2048]{2,1,0:T(8,128)(2,1)}), bf16[8,24,2048]{2,1,0:T(8,128)(2,1)S(1)}, u32[]{:S(2)}, u32[]{:S(2)}) async-start(bf16[8,24,2048]{2,1,0:T(8,128)(2,1)} %bitcast.47), calls=%async_computation.3 | async-start | bytes 1572864 | tf_op jit(solution)/shard_map/all_to_all | solution.py:374
  167.2 3.1 %dynamic_update_slice.3 = bf16[1536,512]{1,0:T(8,128)(2,1)S(1)} dynamic-update-slice(bf16[1536,512]{1,0:T(8,128)(2,1)S(1)} %broadcast_in_dim.15, bf16[512,512]{1,0:T(8,128)(2,1)S(1)} %copy.124, s32[]{:T(128)S(6)} %select_n.59, s32[]{:T(128)} %constant.78.clone.1) | dynamic-update-slice | bytes 1048580 | tf_op jit(solution)/shard_map/dynamic_update_slice | solution.py:328
  170.3 15.7 %all-to-all-done.3 = bf16[8,24,2048]{2,1,0:T(8,128)(2,1)S(1)} async-done(((bf16[8,24,2048]{2,1,0:T(8,128)(2,1)}), bf16[8,24,2048]{2,1,0:T(8,128)(2,1)S(1)}, u32[]{:S(2)}, u32[]{:S(2)}) %all-to-all-start.3) | async-done | bytes 786464 | tf_op jit(solution)/shard_map/all_to_all | solution.py:374
  186.9 28.6 %shard_map.159 = bf16[192,2048]{1,0:T(8,128)(2,1)} custom-call(bf16[192,2048]{1,0:T(8,128)(2,1)} %bitcast.167, bf16[1,2048,5632]{2,1,0:T(8,128)(2,1)} %gate_ref.1, bf16[1,2048,5632]{2,1,0:T(8,128)(2,1)} %up_ref.1, bf16[1,5632,2048]{2,1,0:T(8,128)(2,1)} %down_ref.1), custom_call_target="tpu_custom_call" | custom-call | tf_op jit(solution)/shard_map/pallas_call | solution.py:187
  215.5 3.5 %all-to-all-start.4 = ((bf16[8,24,2048]{2,1,0:T(8,128)(2,1)}), bf16[8,24,2048]{2,1,0:T(8,128)(2,1)S(1)}, u32[]{:S(2)}, u32[]{:S(2)}) async-start(bf16[8,24,2048]{2,1,0:T(8,128)(2,1)} %bitcast.168), calls=%async_computation.4 | async-start | bytes 1572864 | tf_op jit(solution)/shard_map/all_to_all | solution.py:376
  219.0 2.9 %select_bitcast_fusion = bf16[1,1536,512]{2,1,0:T(8,128)(2,1)} fusion(bf16[1536,512]{1,0:T(8,128)(2,1)S(1)} %dynamic_update_slice.3, bf16[1024,512]{1,0:T(8,128)(2,1)} %bitcast.166, pred[1536]{0:T(1024)(128)(4,1)S(1)} %iota_compare_fusion.8), kind=kLoop, calls=%fused_computation.12 | loop fusion | flops 786432 | bytes 4195840 | tf_op jit(solution)/shard_map/broadcast_in_dim | solution.py:383
  222.2 17.7 %all-to-all-done.4 = bf16[8,24,2048]{2,1,0:T(8,128)(2,1)S(1)} async-done(((bf16[8,24,2048]{2,1,0:T(8,128)(2,1)}), bf16[8,24,2048]{2,1,0:T(8,128)(2,1)S(1)}, u32[]{:S(2)}, u32[]{:S(2)}) %all-to-all-start.4) | async-done | bytes 786464 | tf_op jit(solution)/shard_map/all_to_all | solution.py:376
  (133 shorter events, 28.4 us)
Async XLA Ops:
  7.2 101.5 %copy-start = (bf16[2048,8]{0,1:T(8,128)(2,1)S(1)}, bf16[2048,8]{0,1:T(8,128)(2,1)}, u32[]{:S(2)}) copy-start(bf16[2048,8]{0,1:T(8,128)(2,1)} %param.25) | copy-start | bytes 98308
  7.2 40.7 %all-gather.3.cloned.1.call-start = ((), (), s32[]{:S(2)}) async-start(), calls=%async_computation.5 | async-start | bytes 2949120 | tf_op jit(solution)/shard_map/all_gather | solution.py:308
  11.8 4.1 %copy-start.3 = (bf16[1,1024,512]{2,1,0:T(8,128)(2,1)S(1)}, bf16[1,1024,512]{2,1,0:T(8,128)(2,1)}, u32[]{:S(2)}) copy-start(bf16[1,1024,512]{2,1,0:T(8,128)(2,1)} %param.20) | copy-start | bytes 3145732
  52.0 1.2 copy-start.14
  54.4 5.2 %copy-start.13 = (f32[192,64]{1,0:T(8,128)S(1)}, f32[192,64]{1,0:T(8,128)}, u32[]{:S(2)}) copy-start(f32[192,64]{1,0:T(8,128)} %get-tuple-element.32) | copy-start | bytes 147460
  61.6 24.4 %all-to-all-start = ((bf16[8,2,192,128]{3,2,1,0:T(8,128)(2,1)}), bf16[8,2,192,128]{3,2,1,0:T(8,128)(2,1)S(1)}, u32[]{:S(2)}, u32[]{:S(2)}) async-start(bf16[8,2,192,128]{3,2,1,0:T(8,128)(2,1)} %pad_maximum_fusion), calls=%async_computation | async-start | bytes 1572864 | tf_op jit(solution)/shard_map/all_to_all | solution.py:344
  65.1 3.9 %copy-start.15 = (s32[8,8,24]{2,1,0:T(8,128)S(1)}, s32[8,8,24]{2,1,0:T(8,128)}, u32[]{:S(2)}) copy-start(s32[8,8,24]{2,1,0:T(8,128)} %copy-done.14) | copy-start | bytes 18436
  69.0 2.3 copy-start.12
  69.0 2.3 copy-start.11
  71.6 1.0 copy-start.9
  71.6 1.2 copy-start.10
  100.7 5.8 %copy-start.17 = (s32[1,64,2]{1,2,0:T(2,128)S(1)}, s32[1,64,2]{1,2,0:T(2,128)}, u32[]{:S(2)}) copy-start(s32[1,64,2]{1,2,0:T(2,128)} %param.22) | copy-start | bytes 1540
  102.8 24.5 %all-to-all-start.1 = ((bf16[8,2,192,128]{3,2,1,0:T(8,128)(2,1)}), bf16[8,2,192,128]{3,2,1,0:T(8,128)(2,1)S(1)}, u32[]{:S(2)}, u32[]{:S(2)}) async-start(bf16[8,2,192,128]{3,2,1,0:T(8,128)(2,1)} %bitcast.152), calls=%async_computation.1 | async-start | bytes 1572864 | tf_op jit(solution)/shard_map/all_to_all | solution.py:355
  107.0 1.2 copy-start.18
  132.8 24.5 %all-to-all-start.2 = ((bf16[8,24,2048]{2,1,0:T(8,128)(2,1)}), bf16[8,24,2048]{2,1,0:T(8,128)(2,1)S(1)}, u32[]{:S(2)}, u32[]{:S(2)}) async-start(bf16[8,24,2048]{2,1,0:T(8,128)(2,1)} %bitcast.35), calls=%async_computation.2 | async-start | bytes 1572864 | tf_op jit(solution)/shard_map/all_to_all | solution.py:359
  158.0 1.4 copy-start.5
  158.0 1.0 copy-start.2
  158.0 1.4 copy-start.19
  158.8 2.8 %copy-start.7 = (bf16[64,2048]{1,0:T(8,128)(2,1)}, bf16[64,2048]{1,0:T(8,128)(2,1)S(1)}, u32[]{:S(2)}) copy-start(bf16[64,2048]{1,0:T(8,128)(2,1)S(1)} %gather_fusion.2) | copy-start | bytes 786436
  161.5 24.5 %all-to-all-start.3 = ((bf16[8,24,2048]{2,1,0:T(8,128)(2,1)}), bf16[8,24,2048]{2,1,0:T(8,128)(2,1)S(1)}, u32[]{:S(2)}, u32[]{:S(2)}) async-start(bf16[8,24,2048]{2,1,0:T(8,128)(2,1)} %bitcast.47), calls=%async_computation.3 | async-start | bytes 1572864 | tf_op jit(solution)/shard_map/all_to_all | solution.py:374
  215.5 24.4 %all-to-all-start.4 = ((bf16[8,24,2048]{2,1,0:T(8,128)(2,1)}), bf16[8,24,2048]{2,1,0:T(8,128)(2,1)S(1)}, u32[]{:S(2)}, u32[]{:S(2)}) async-start(bf16[8,24,2048]{2,1,0:T(8,128)(2,1)} %bitcast.168), calls=%async_computation.4 | async-start | bytes 1572864 | tf_op jit(solution)/shard_map/all_to_all | solution.py:376
  219.0 2.9 %copy-start.16 = (bf16[2048,8]{0,1:T(8,128)(2,1)S(1)}, bf16[2048,8]{0,1:T(8,128)(2,1)}, u32[]{:S(2)}) copy-start(bf16[2048,8]{0,1:T(8,128)(2,1)} %param.30) | copy-start | bytes 98308
  240.7 1.0 copy-start.8
  240.7 2.0 copy-start.1
  (2 other events, 1.8 us)
Sparse Core Ops, SparseCore 0:
  11.3 36.5 all-gather.2

commit v4 on v2

--- a/solution.py
+++ b/solution.py
@@ -1,3 +1,4 @@
+import functools
 import math
 
 import jax
@@ -197,6 +198,75 @@
         scratch_shapes=[pltpu.VMEM((row_count, width), jnp.float32)],
         compiler_params=pltpu.CompilerParams(dimension_semantics=("arbitrary",)),
     )(rows, w_gate, w_up, w_down)
+
+
+def attention_kernel(
+    length_ref, query_ref, pos_ref, cache_key_ref, cache_value_ref, fresh_key_ref,
+    fresh_value_ref, out_ref,
+):
+    length = length_ref[0]
+    queries = query_ref[...]
+    factor = queries.shape[-1] ** (-0.5)
+    contract = (((1,), (1,)), ((), ()))
+    cache_scores = (
+        lax.dot_general(queries, cache_key_ref[...], contract, preferred_element_type=jnp.float32)
+        * factor
+    )
+    fresh_scores = (
+        lax.dot_general(queries, fresh_key_ref[...], contract, preferred_element_type=jnp.float32)
+        * factor
+    )
+    cache_column = lax.broadcasted_iota(jnp.int32, cache_scores.shape, 1)
+    fresh_column = lax.broadcasted_iota(jnp.int32, fresh_scores.shape, 1)
+    cache_scores = jnp.where(cache_column < length, cache_scores, masked_score)
+    fresh_scores = jnp.where(fresh_column <= pos_ref[...], fresh_scores, masked_score)
+    top = jnp.maximum(
+        jnp.max(cache_scores, axis=1, keepdims=True), jnp.max(fresh_scores, axis=1, keepdims=True)
+    )
+    cache_weights = jnp.exp(cache_scores - top)
+    fresh_weights = jnp.exp(fresh_scores - top)
+    total = jnp.sum(cache_weights, axis=1, keepdims=True) + jnp.sum(
+        fresh_weights, axis=1, keepdims=True
+    )
+    summed = jnp.dot(
+        cache_weights.astype(jnp.bfloat16), cache_value_ref[...], preferred_element_type=jnp.float32
+    ) + jnp.dot(
+        fresh_weights.astype(jnp.bfloat16), fresh_value_ref[...], preferred_element_type=jnp.float32
+    )
+    out_ref[...] = (summed / total).astype(out_ref.dtype)
+
+
+def kernel_attention(queries, query_pos, cache, fresh, length):
+    expert_count, head_count, slot_count, head_dim = queries.shape
+    cache_rows = cache.shape[0]
+    fresh_rows = fresh.shape[0]
+    grid_spec = pltpu.PrefetchScalarGridSpec(
+        num_scalar_prefetch=1,
+        grid=(head_count, expert_count),
+        in_specs=[
+            pl.BlockSpec((None, None, slot_count, head_dim), lambda h, a, n: (a, h, 0, 0)),
+            pl.BlockSpec((None, slot_count, 1), lambda h, a, n: (a, 0, 0)),
+            pl.BlockSpec((cache_rows, head_dim), lambda h, a, n: (0, 2 * h)),
+            pl.BlockSpec((cache_rows, head_dim), lambda h, a, n: (0, 2 * h + 1)),
+            pl.BlockSpec((fresh_rows, head_dim), lambda h, a, n: (0, 2 * h)),
+            pl.BlockSpec((fresh_rows, head_dim), lambda h, a, n: (0, 2 * h + 1)),
+        ],
+        out_specs=pl.BlockSpec((None, None, slot_count, head_dim), lambda h, a, n: (a, h, 0, 0)),
+    )
+    return pl.pallas_call(
+        attention_kernel,
+        grid_spec=grid_spec,
+        out_shape=jax.ShapeDtypeStruct(queries.shape, jnp.bfloat16),
+        compiler_params=pltpu.CompilerParams(dimension_semantics=("arbitrary", "arbitrary")),
+    )(
+        jnp.reshape(length, (1,)).astype(jnp.int32),
+        queries,
+        query_pos.reshape(expert_count, slot_count, 1),
+        cache,
+        cache,
+        fresh,
+        fresh,
+    )
 
 
 def head_attention(queries, query_pos, keys, values, length, cache_limit):
@@ -261,14 +331,16 @@
     gathered = lax.all_gather(
         jnp.concatenate([normed, route_rows], axis=0), "exp", axis=0, tiled=False
     )
-    group_normed = gathered[:, :rows_block].reshape(-1, model_width)
+    stride = gathered.shape[1]
+    gathered_flat = gathered.reshape(-1, model_width)
     group_routes = (
         gathered[:, rows_block, : 2 * rows_block].astype(jnp.int32).reshape(-1, 2)
     )
-    row_total = group_normed.shape[0]
-    block_count = row_total // rows_block
+    block_count = gathered.shape[0]
+    row_total = block_count * rows_block
     new_pos = length + jnp.arange(row_total, dtype=jnp.int32)
-    fresh_kv = jnp.dot(group_normed, w_keyval, preferred_element_type=jnp.float32)
+    fresh_kv = jnp.dot(gathered_flat, w_keyval, preferred_element_type=jnp.float32)
+    fresh_kv = fresh_kv.reshape(block_count, stride, columns)[:, :rows_block].reshape(row_total, columns)
     split_new = fresh_kv.reshape(row_total, columns // (2 * head_dim), 2, head_dim)
     rotated = rotate(split_new[:, :, 0], new_pos[:, None])
     fresh_kv = (
@@ -288,23 +360,14 @@
     slot_tokens = slot_tokens + (jnp.arange(block_count, dtype=jnp.int32) * rows_block)[:, None, None]
     expert_tokens = jnp.swapaxes(slot_tokens, 0, 1).reshape(experts_attn, -1)
     my_tokens = expert_tokens[position]
-    picked_rows = group_normed[my_tokens]
+    picked_rows = gathered_flat[my_tokens // rows_block * stride + my_tokens % rows_block]
     queries = jnp.einsum("sd,hdk->hsk", picked_rows, w_query, preferred_element_type=jnp.float32)
     queries = rotate(queries, (length + my_tokens)[None, :]).astype(jnp.bfloat16)
     heads_local = columns // (2 * head_dim)
     query_slots = queries.shape[1]
     send_q = queries.reshape(device_count, heads_local, query_slots, head_dim)
     recv_q = lax.all_to_all(send_q, "exp", 0, 0, tiled=True)
-    recv_q = jnp.swapaxes(recv_q, 0, 1).reshape(heads_local, device_count * query_slots, head_dim)
-    query_pos = expert_tokens.reshape(-1)
-    split_old = cache[0].reshape(cache_limit, heads_local, 2, head_dim)
-    split_fresh = fresh_kv.reshape(row_total, heads_local, 2, head_dim)
-    keys = jnp.swapaxes(jnp.concatenate([split_old[:, :, 0], split_fresh[:, :, 0]], axis=0), 0, 1)
-    values = jnp.swapaxes(jnp.concatenate([split_old[:, :, 1], split_fresh[:, :, 1]], axis=0), 0, 1)
-    head_outs = head_attention(recv_q, query_pos, keys, values, length, cache_limit)
-    send_o = jnp.swapaxes(
-        head_outs.reshape(heads_local, device_count, query_slots, head_dim), 0, 1
-    )
+    send_o = kernel_attention(recv_q, expert_tokens, cache[0], fresh_kv, length)
     recv_o = lax.all_to_all(send_o, "exp", 0, 0, tiled=True)
     recv_o = recv_o.reshape(heads_here, query_slots, head_dim)
     projected = jnp.einsum("hsk,hkd->sd", recv_o, w_out, preferred_element_type=jnp.float32)

time: 263 us -> 254 us (0.966)
  matrix products: 31.9 us -> 15.2 us
  Pallas kernels: 28.6 us -> 44.8 us
  other arithmetic: 23.4 us -> 19.1 us
  local copies, waits for them, and re-layouts: 29.9 us -> 27.2 us
    dot_general x3 -> x1, matrix products: 20.2 us -> 3.81 us  [body(): jnp.dot(gathered_flat, w_keyval, preferred_element_type=jnp.float32)]
    pallas_call x0 -> x1, Pallas kernels: none -> 16.2 us  [kernel_attention(): pl.pallas_call(attention_kernel, grid_spec=grid_spec, out_shape=jax.Shape...]
    all_to_all x1, waiting for transfers between devices: 15.4 us -> 5.96 us  [body(): recv_q = lax.all_to_all(send_q, 'exp', 0, 0, tiled=True)]
    all_gather x1, waiting for transfers between devices: 28.2 us -> 36.1 us  [body(): lax.all_gather(jnp.concatenate([normed, route_rows], axis=0), 'exp', axis...]
    reduce_sum x1 -> x0, other arithmetic: 6.51 us -> none  [head_attention(): total = jnp.sum(weights, axis=-1, keepdims=True)]
    dot_general x1 -> x0, local copies, waits for them, and re-layouts: 3.96 us -> none  [body(): jnp.dot(group_normed, w_keyval, preferred_element_type=jnp.float32)]
    another operation x0 -> x3, local copies, waits for them, and re-layouts: none -> 3.57 us  [the longest x1 1.88 us: body(): fresh_kv.reshape(row_total, columns // (2 * head_dim), 2, head_dim)]
    select_n x2 -> x1, other arithmetic: 3.33 us -> 0.02 us  [body(): gathered_flat[my_tokens // rows_block * stride + my_tokens % rows_block]]
  transfers between devices with their start and end apart: 6 -> 6, of which waited for: 6 -> 6; matrix products, arithmetic and copies ran while one was open for 10% -> 11% of each run, Pallas kernels for 0% -> 0%
where the time goes in v4:
time: 254 us; the launch traced here: 253 us
  waiting for transfers between devices  113 us (44%)
  Pallas kernels  44.8 us (18%)
  local copies, waits for them, and re-layouts  27.2 us (11%)
  other arithmetic  19.1 us (8%)
  starting transfers between devices  18.4 us (7%)
  matrix products  15.2 us (6%)
  between operations  15.2 us (6%)
    all_gather x1, waiting for transfers between devices, body(): lax.all_gather(jnp.concatenate([normed, route_rows], axis=0), 'exp', axis...  36.1 us
    pallas_call x1, Pallas kernels, expert_mlp(): pl.pallas_call(mlp_kernel, grid=(hidden_units // tile,), in_specs=[pl.Blo...  28.6 us
    all_to_all x1, waiting for transfers between devices, body(): recv_p = lax.all_to_all(send_p, 'exp', 0, 0, tiled=True)  20.8 us
    all_to_all x1, waiting for transfers between devices, body(): recv_o = lax.all_to_all(send_o, 'exp', 0, 0, tiled=True)  18.5 us
    all_to_all x1, waiting for transfers between devices, body(): lax.all_to_all(slice_out.reshape(device_count, slot_count, model_width),...  17.5 us
    pallas_call x1, Pallas kernels, kernel_attention(): pl.pallas_call(attention_kernel, grid_spec=grid_spec, out_shape=jax.Shape...  16.2 us
    all_to_all x1, waiting for transfers between devices, body(): lax.all_to_all(send_m, 'exp', 0, 0, tiled=True).reshape(-1, model_width)  14 us
    all_to_all x1, waiting for transfers between devices, body(): recv_q = lax.all_to_all(send_q, 'exp', 0, 0, tiled=True)  5.96 us
  transfers between devices with their start and end apart: 6, of which 6 were waited for; matrix products, arithmetic and copies ran while one was open for 11% of the time, Pallas kernels for 0%

profile of v4, /device:TPU:0, one launch (start us, length us, event | category | flops | bytes accessed | tf_op | source)
XLA Modules:
  0.0 252.7 jit_solution(3689848255231368052)
XLA Ops:
  12.0 36.1 %all-gather.3.cloned.1.call-done = bf16[640,2048]{1,0:T(8,128)(2,1)} async-done(((bf16[80,2048]{1,0:T(8,128)(2,1)}), bf16[640,2048]{1,0:T(8,128)(2,1)}) %all-gather.3.cloned.1.call-update) | async-done | bytes 2621456 | tf_op jit(solution)/shard_map/all_gather | solution.py:331
  51.0 4.0 %gather_fusion = bf16[192,2048]{1,0:T(8,128)(2,1)S(1)} fusion(bf16[640,2048]{1,0:T(8,128)(2,1)} %all-gather.3.cloned.1.call-done, s32[1024]{0:T(1024)S(1)} %pad_clamp_fusion.5), kind=kCustom, calls=%fused_computation.2 | custom fusion | bytes 1573632 | tf_op jit(solution)/shard_map/gather | solution.py:363
  54.9 5.2 %convolution_bitcast_fusion.1 = f32[16,192,128]{2,1,0:T(8,128)S(1)} fusion(bf16[16,2048,128]{2,1,0:T(8,128)(2,1)} %param.26, bf16[192,2048]{1,0:T(8,128)(2,1)S(1)} %gather_fusion), kind=kOutput, calls=%fused_computation.16 | convolution fusion | flops 1610612736 | bytes 10747904 | tf_op jit(solution)/shard_map/sd,hdk->hsk/dot_general | solution.py:364
  62.1 3.7 %all-to-all-start = ((bf16[8,2,192,128]{3,2,1,0:T(8,128)(2,1)}), bf16[8,2,192,128]{3,2,1,0:T(8,128)(2,1)S(1)}, u32[]{:S(2)}, u32[]{:S(2)}) async-start(bf16[8,2,192,128]{3,2,1,0:T(8,128)(2,1)} %pad_maximum_fusion), calls=%async_computation | async-start | bytes 1572864 | tf_op jit(solution)/shard_map/all_to_all | solution.py:369
  65.8 1.8 multiply_cosine_fusion
  67.6 3.8 %fusion.1 = f32[8,64,512]{2,1,0:T(8,128)} fusion(bf16[8,80,2048]{2,1,0:T(8,128)(2,1)} %bitcast.154, bf16[2048,512]{1,0:T(8,128)(2,1)S(1)} %copy-done), kind=kOutput, calls=%fused_computation.10 | convolution fusion | flops 1073741824 | bytes 5242880 | tf_op jit(solution)/shard_map/dot_general | solution.py:342
  71.4 1.9 reshape_reshape.7
  75.4 1.7 subtract_convert_fusion.1
  80.6 6.0 %all-to-all-done.query_ref = bf16[8,2,192,128]{3,2,1,0:T(8,128)(2,1)S(1)} async-done(((bf16[8,2,192,128]{3,2,1,0:T(8,128)(2,1)}), bf16[8,2,192,128]{3,2,1,0:T(8,128)(2,1)S(1)}, u32[]{:S(2)}, u32[]{:S(2)}) %all-to-all-start) | async-done | bytes 786464 | tf_op jit(solution)/shard_map/all_to_all | solution.py:369
  87.4 16.2 %shard_map.158 = bf16[8,2,192,128]{3,2,1,0:T(8,128)(2,1)} custom-call(s32[1]{0:T(128)} %copy.94.length_ref, bf16[8,2,192,128]{3,2,1,0:T(8,128)(2,1)} %copy-done.6, s32[8,192,1]{2,1,0:T(8,128)} %reshape_reshape.8.pos_ref, bf16[1024,512]{1,0:T(8,128)(2,1)} %bitcast.155, bf16[1024,512]{1,0:T(8,128)(2,1)} %bitcast.156, ...), custom_call_target="tpu_custom_call" | custom-call | tf_op jit(solution)/shard_map/pallas_call | solution.py:256
  103.6 3.7 %all-to-all-start.1 = ((bf16[8,2,192,128]{3,2,1,0:T(8,128)(2,1)}), bf16[8,2,192,128]{3,2,1,0:T(8,128)(2,1)S(1)}, u32[]{:S(2)}, u32[]{:S(2)}) async-start(bf16[8,2,192,128]{3,2,1,0:T(8,128)(2,1)} %shard_map.158), calls=%async_computation.1 | async-start | bytes 1572864 | tf_op jit(solution)/shard_map/all_to_all | solution.py:371
  109.6 18.5 %all-to-all-done.1 = bf16[8,2,192,128]{3,2,1,0:T(8,128)(2,1)S(1)} async-done(((bf16[8,2,192,128]{3,2,1,0:T(8,128)(2,1)}), bf16[8,2,192,128]{3,2,1,0:T(8,128)(2,1)S(1)}, u32[]{:S(2)}, u32[]{:S(2)}) %all-to-all-start.1) | async-done | bytes 786464 | tf_op jit(solution)/shard_map/all_to_all | solution.py:371
  128.2 5.5 %fusion = bf16[192,2048]{1,0:T(8,128)(2,1)} fusion(bf16[16,192,128]{2,1,0:T(8,128)(2,1)S(1)} %bitcast.163, bf16[16,128,2048]{2,1,0:T(8,128)(2,1)} %param.28), kind=kOutput, calls=%fused_computation.9 | convolution fusion | flops 1611005952 | bytes 9961472 | tf_op jit(solution)/shard_map/hsk,hkd->sd/dot_general | solution.py:373
  133.7 3.5 %all-to-all-start.2 = ((bf16[8,24,2048]{2,1,0:T(8,128)(2,1)}), bf16[8,24,2048]{2,1,0:T(8,128)(2,1)S(1)}, u32[]{:S(2)}, u32[]{:S(2)}) async-start(bf16[8,24,2048]{2,1,0:T(8,128)(2,1)} %bitcast.22), calls=%async_computation.2 | async-start | bytes 1572864 | tf_op jit(solution)/shard_map/all_to_all | solution.py:375
  137.3 20.8 %all-to-all-done.2 = bf16[8,24,2048]{2,1,0:T(8,128)(2,1)S(1)} async-done(((bf16[8,24,2048]{2,1,0:T(8,128)(2,1)}), bf16[8,24,2048]{2,1,0:T(8,128)(2,1)S(1)}, u32[]{:S(2)}, u32[]{:S(2)}) %all-to-all-start.2) | async-done | bytes 786464 | tf_op jit(solution)/shard_map/all_to_all | solution.py:375
  160.3 2.0 gather_fusion.3
  162.3 3.8 %all-to-all-start.3 = ((bf16[8,24,2048]{2,1,0:T(8,128)(2,1)}), bf16[8,24,2048]{2,1,0:T(8,128)(2,1)S(1)}, u32[]{:S(2)}, u32[]{:S(2)}) async-start(bf16[8,24,2048]{2,1,0:T(8,128)(2,1)} %bitcast.34), calls=%async_computation.3 | async-start | bytes 1572864 | tf_op jit(solution)/shard_map/all_to_all | solution.py:390
  168.9 3.9 %dynamic_update_slice.3 = bf16[1536,512]{1,0:T(8,128)(2,1)} dynamic-update-slice(bf16[1536,512]{1,0:T(8,128)(2,1)} %broadcast_in_dim.15, bf16[512,512]{1,0:T(8,128)(2,1)S(1)} %copy-done.3, s32[]{:T(128)S(6)} %select_n.87, s32[]{:T(128)} %constant.101.clone.1) | dynamic-update-slice | bytes 1048580 | tf_op jit(solution)/shard_map/dynamic_update_slice | solution.py:353
  172.8 14.0 %all-to-all-done.3 = bf16[8,24,2048]{2,1,0:T(8,128)(2,1)S(1)} async-done(((bf16[8,24,2048]{2,1,0:T(8,128)(2,1)}), bf16[8,24,2048]{2,1,0:T(8,128)(2,1)S(1)}, u32[]{:S(2)}, u32[]{:S(2)}) %all-to-all-start.3) | async-done | bytes 786464 | tf_op jit(solution)/shard_map/all_to_all | solution.py:390
  187.6 28.6 %shard_map.159 = bf16[192,2048]{1,0:T(8,128)(2,1)} custom-call(bf16[192,2048]{1,0:T(8,128)(2,1)} %bitcast.159, bf16[1,2048,5632]{2,1,0:T(8,128)(2,1)} %gate_ref.1, bf16[1,2048,5632]{2,1,0:T(8,128)(2,1)} %up_ref.1, bf16[1,5632,2048]{2,1,0:T(8,128)(2,1)} %down_ref.1), custom_call_target="tpu_custom_call" | custom-call | tf_op jit(solution)/shard_map/pallas_call | solution.py:187
  216.3 3.7 %all-to-all-start.4 = ((bf16[8,24,2048]{2,1,0:T(8,128)(2,1)}), bf16[8,24,2048]{2,1,0:T(8,128)(2,1)S(1)}, u32[]{:S(2)}, u32[]{:S(2)}) async-start(bf16[8,24,2048]{2,1,0:T(8,128)(2,1)} %bitcast.160), calls=%async_computation.4 | async-start | bytes 1572864 | tf_op jit(solution)/shard_map/all_to_all | solution.py:392
  220.0 3.1 %select_bitcast_fusion = bf16[1,1536,512]{2,1,0:T(8,128)(2,1)} fusion(bf16[1536,512]{1,0:T(8,128)(2,1)} %dynamic_update_slice.3, bf16[1024,512]{1,0:T(8,128)(2,1)S(1)} %bitcast.157, pred[1536]{0:T(1024)(128)(4,1)S(1)} %iota_compare_fusion.8), kind=kLoop, calls=%fused_computation.13 | loop fusion | flops 786432 | bytes 4195840 | tf_op jit(solution)/shard_map/broadcast_in_dim | solution.py:399
  223.3 17.5 %all-to-all-done.4 = bf16[8,24,2048]{2,1,0:T(8,128)(2,1)S(1)} async-done(((bf16[8,24,2048]{2,1,0:T(8,128)(2,1)}), bf16[8,24,2048]{2,1,0:T(8,128)(2,1)S(1)}, u32[]{:S(2)}, u32[]{:S(2)}) %all-to-all-start.4) | async-done | bytes 786464 | tf_op jit(solution)/shard_map/all_to_all | solution.py:392
  243.7 2.1 fusion.29
  (110 shorter events, 26.6 us)
Async XLA Ops:
  7.2 60.4 %copy-start = (bf16[2048,512]{1,0:T(8,128)(2,1)S(1)}, bf16[2048,512]{1,0:T(8,128)(2,1)}, u32[]{:S(2)}) copy-start(bf16[2048,512]{1,0:T(8,128)(2,1)} %param.27) | copy-start | bytes 6291460
  7.2 40.9 %all-gather.3.cloned.1.call-start = ((), (), s32[]{:S(2)}) async-start(), calls=%async_computation.5 | async-start | bytes 2949120 | tf_op jit(solution)/shard_map/all_gather | solution.py:331
  62.1 24.5 %all-to-all-start = ((bf16[8,2,192,128]{3,2,1,0:T(8,128)(2,1)}), bf16[8,2,192,128]{3,2,1,0:T(8,128)(2,1)S(1)}, u32[]{:S(2)}, u32[]{:S(2)}) async-start(bf16[8,2,192,128]{3,2,1,0:T(8,128)(2,1)} %pad_maximum_fusion), calls=%async_computation | async-start | bytes 1572864 | tf_op jit(solution)/shard_map/all_to_all | solution.py:369
  86.5 0.9 copy-start.6
  103.6 3.7 %copy-start.10 = (s32[1,64,2]{1,2,0:T(2,128)S(1)}, s32[1,64,2]{1,2,0:T(2,128)}, u32[]{:S(2)}) copy-start(s32[1,64,2]{1,2,0:T(2,128)} %param.22) | copy-start | bytes 1540
  103.6 24.6 %all-to-all-start.1 = ((bf16[8,2,192,128]{3,2,1,0:T(8,128)(2,1)}), bf16[8,2,192,128]{3,2,1,0:T(8,128)(2,1)S(1)}, u32[]{:S(2)}, u32[]{:S(2)}) async-start(bf16[8,2,192,128]{3,2,1,0:T(8,128)(2,1)} %shard_map.158), calls=%async_computation.1 | async-start | bytes 1572864 | tf_op jit(solution)/shard_map/all_to_all | solution.py:371
  107.7 1.2 copy-start.11
  107.7 1.7 copy-start.8
  133.7 24.5 %all-to-all-start.2 = ((bf16[8,24,2048]{2,1,0:T(8,128)(2,1)}), bf16[8,24,2048]{2,1,0:T(8,128)(2,1)S(1)}, u32[]{:S(2)}, u32[]{:S(2)}) async-start(bf16[8,24,2048]{2,1,0:T(8,128)(2,1)} %bitcast.22), calls=%async_computation.2 | async-start | bytes 1572864 | tf_op jit(solution)/shard_map/all_to_all | solution.py:375
  158.9 1.0 copy-start.4
  158.9 1.3 copy-start.12
  159.6 2.7 %copy-start.7 = (bf16[64,2048]{1,0:T(8,128)(2,1)}, bf16[64,2048]{1,0:T(8,128)(2,1)S(1)}, u32[]{:S(2)}) copy-start(bf16[64,2048]{1,0:T(8,128)(2,1)S(1)} %gather_fusion.2) | copy-start | bytes 786436
  162.3 24.5 %all-to-all-start.3 = ((bf16[8,24,2048]{2,1,0:T(8,128)(2,1)}), bf16[8,24,2048]{2,1,0:T(8,128)(2,1)S(1)}, u32[]{:S(2)}, u32[]{:S(2)}) async-start(bf16[8,24,2048]{2,1,0:T(8,128)(2,1)} %bitcast.34), calls=%async_computation.3 | async-start | bytes 1572864 | tf_op jit(solution)/shard_map/all_to_all | solution.py:390
  167.4 1.5 copy-start.3
  186.8 0.9 copy-start.5
  216.2 3.7 %copy-start.2 = (bf16[1,1024,512]{2,1,0:T(8,128)(2,1)S(1)}, bf16[1,1024,512]{2,1,0:T(8,128)(2,1)}, u32[]{:S(2)}) copy-start(bf16[1,1024,512]{2,1,0:T(8,128)(2,1)} %param.20) | copy-start | bytes 3145732
  216.3 24.6 %all-to-all-start.4 = ((bf16[8,24,2048]{2,1,0:T(8,128)(2,1)}), bf16[8,24,2048]{2,1,0:T(8,128)(2,1)S(1)}, u32[]{:S(2)}, u32[]{:S(2)}) async-start(bf16[8,24,2048]{2,1,0:T(8,128)(2,1)} %bitcast.160), calls=%async_computation.4 | async-start | bytes 1572864 | tf_op jit(solution)/shard_map/all_to_all | solution.py:392
  219.9 3.1 %copy-start.9 = (bf16[2048,8]{0,1:T(8,128)(2,1)S(1)}, bf16[2048,8]{0,1:T(8,128)(2,1)}, u32[]{:S(2)}) copy-start(bf16[2048,8]{0,1:T(8,128)(2,1)} %param.30) | copy-start | bytes 98308
  242.3 3.6 %copy-start.1 = (bf16[2048,512]{1,0:T(8,128)(2,1)S(1)}, bf16[2048,512]{1,0:T(8,128)(2,1)}, u32[]{:S(2)}) copy-start(bf16[2048,512]{1,0:T(8,128)(2,1)} %param.27) | copy-start | bytes 6291460
Sparse Core Ops, SparseCore 0:
  11.4 36.5 all-gather.2
